TPU v7x, 32 devices: a whole 2x2x4 slice. The times are simulated.
32 devices in a mesh: groups: 2 (over x), blocks: 16 (over z, y, core).
Axes of the slice: x: 2, y: 2, z: 4, core: 2. Of those that a mesh axis runs over, the one named last changes fastest.
Arguments:
- source_coords: bfloat16 [30, 32768], P(None, ('groups', 'blocks')), parts along dimension 1
- target_coords: bfloat16 [30, 32768], P(None, ('groups', 'blocks')), parts along dimension 1
- target_potential: float32 [32768], P(('groups', 'blocks')), parts along dimension 0, may hold values from -8 to 8
- fetch_blocks: int32 [32, 16, 2], P(('groups', 'blocks')), parts along dimension 0, may hold values from 0 to 127, as said below
- pair_slots: int32 [256, 32], P(('groups', 'blocks')), parts along dimension 0, may hold values from 0 to 31, as said below
- pair_counts: int32 [256], P(('groups', 'blocks')), parts along dimension 0, may hold values from 1 to 32
Outputs:
- source_potential: float32 [32768], P(('groups', 'blocks')), parts along dimension 0
- target_potential_out: float32 [32768], P(('groups', 'blocks')), parts along dimension 0
- drift: float32 [30, 32768], P(None, ('groups', 'blocks')), parts along dimension 1
There are 2 independent parts, one for each index of `groups`. A program takes and returns all parts, laid end to end along the dimension named above; each array names one. Nothing has to cross between parts.
Inputs may be any that keep to these rules, and one draw needn't show every extreme that they name: `fetch_blocks`: entry [d, o, c] is a target block owned by device o, that is between o * 8 and o * 8 + 7; the 2 entries of one [d, o] are distinct. `pair_slots`: entry [s, p] names entry (o, c) of the fetch list of device s // 8 as o * 2 + c; the 32 entries of a row are distinct; entries at p >= pair_counts[s] are unused.
All inputs are finite; a program needn't handle non-finite values.
Results may differ from a plain program's by a relative error of at most 0.00095.
Values may be sent and summed in bfloat16 or wider, within the bound.
No kernel may reach another device: no remote copies, remote signals or barrier semaphores. Data moves between devices by JAX's collectives and lax.ppermute only.
A program may use at most 64 MiB of HBM per device.

v0:
```python
import functools
import math

import jax
import jax.numpy as jnp
from jax import lax
from jax.experimental import pallas as pl
from jax.experimental.pallas import tpu as pltpu
from jax.sharding import PartitionSpec as P

SWEEPS = 2

floor_value = -1e30
PADDED = 32
CHUNK = 8


def _chunk_slots(slots_ref, s, q, most):
    return [slots_ref[s * most + jnp.minimum(q * CHUNK + c, most - 1)] for c in range(CHUNK)]


def _rows_of(values):
    return jnp.concatenate(values, axis=0)


def _row_scores(s, cnt, slots_ref, xs, y_ref, h_ref, s_ref, most, bs):
    lane_tile = lax.broadcasted_iota(jnp.int32, (1, CHUNK * bs), 1) // bs

    def first(q, m):
        sls = _chunk_slots(slots_ref, s, q, most)
        rhs = jnp.concatenate([y_ref[sl] for sl in sls], axis=1)
        hrow = jnp.concatenate([h_ref[sl] for sl in sls], axis=1)
        hrow = jnp.where(lane_tile + q * CHUNK < cnt, hrow, floor_value)
        sc = jnp.dot(xs, rhs, preferred_element_type=jnp.float32) + hrow
        for t in range(CHUNK):
            tile = sc[:, t * bs : (t + 1) * bs]
            s_ref[q, :, t * bs : (t + 1) * bs] = tile
            m = jnp.maximum(m, tile)
        return m

    nq = (cnt + CHUNK - 1) // CHUNK
    m = lax.fori_loop(0, nq, first, jnp.full((bs, bs), floor_value, jnp.float32))
    return nq, jnp.max(m, axis=1, keepdims=True)


def sweep_kernel(slots_ref, counts_ref, xT_ref, y_ref, h_ref, g_ref, lse_ref, amax_ref, asum_ref, s_ref, *, most, log_mass):
    nblk, bs = xT_ref.shape[0], xT_ref.shape[1]
    amax_ref[...] = jnp.full(amax_ref.shape, floor_value, jnp.float32)
    asum_ref[...] = jnp.zeros(asum_ref.shape, jnp.float32)
    tile_row = lax.broadcasted_iota(jnp.int32, (CHUNK, bs), 0)

    def block(s, carry):
        cnt = counts_ref[s]
        nq, mrow = _row_scores(s, cnt, slots_ref, xT_ref[s], y_ref, h_ref, s_ref, most, bs)
        mb = jnp.broadcast_to(mrow, (bs, bs))

        def second(q, acc):
            for t in range(CHUNK):
                acc = acc + jnp.exp(s_ref[q, :, t * bs : (t + 1) * bs] - mb)
            return acc

        acc = lax.fori_loop(0, nq, second, jnp.zeros((bs, bs), jnp.float32))
        tot = jnp.sum(acc, axis=1, keepdims=True)
        kb = jnp.broadcast_to(log_mass - (mrow + jnp.log(tot)), (bs, bs))

        def column(q, c):
            sls = _chunk_slots(slots_ref, s, q, most)
            cms, ces = [], []
            for t in range(CHUNK):
                v = s_ref[q, :, t * bs : (t + 1) * bs] + kb
                cm = jnp.max(v, axis=0, keepdims=True)
                cms.append(cm)
                ces.append(jnp.sum(jnp.exp(v - cm), axis=0, keepdims=True))
            valid = tile_row + q * CHUNK < cnt
            tm = jnp.where(valid, _rows_of(cms) - _rows_of([g_ref[sl] for sl in sls]), floor_value)
            te = jnp.where(valid, _rows_of(ces), 0.0)
            om = _rows_of([amax_ref[sl] for sl in sls])
            os = _rows_of([asum_ref[sl] for sl in sls])
            nm = jnp.maximum(om, tm)
            ns = os * jnp.exp(om - nm) + te * jnp.exp(tm - nm)
            for t, sl in enumerate(sls):
                amax_ref[sl] = nm[t : t + 1]
                asum_ref[sl] = ns[t : t + 1]
            return c

        lax.fori_loop(0, nq, column, 0)
        return carry

    lax.fori_loop(0, nblk, block, 0)

    am = amax_ref[...]
    lse_ref[...] = jnp.where(am > 0.5 * floor_value, am + jnp.log(asum_ref[...]), floor_value)


def final_kernel(slots_ref, counts_ref, xT_ref, x_ref, y_ref, yT_ref, h_ref, f_ref, drift_ref, s_ref, *, most, log_mass, ncomp):
    nblk, bs = xT_ref.shape[0], xT_ref.shape[1]
    lanes = lax.broadcasted_iota(jnp.int32, (bs, yT_ref.shape[2]), 1)

    def block(s, carry):
        cnt = counts_ref[s]
        xs = xT_ref[s]
        nq, mrow = _row_scores(s, cnt, slots_ref, xs, y_ref, h_ref, s_ref, most, bs)
        mb = jnp.broadcast_to(mrow, (bs, bs))

        def second(q, c):
            acc, num = c
            sls = _chunk_slots(slots_ref, s, q, most)
            for t, sl in enumerate(sls):
                e = jnp.exp(s_ref[q, :, t * bs : (t + 1) * bs] - mb)
                acc = acc + e
                num = num + jnp.dot(e.astype(jnp.bfloat16), yT_ref[sl], preferred_element_type=jnp.float32)
            return acc, num

        acc, num = lax.fori_loop(
            0,
            nq,
            second,
            (jnp.zeros((bs, bs), jnp.float32), jnp.zeros((bs, yT_ref.shape[2]), jnp.float32)),
        )
        tot = jnp.sum(acc, axis=1, keepdims=True)
        xf = xs.astype(jnp.float32)
        quarter_nx = jnp.sum(xf * xf, axis=1, keepdims=True)
        fcol = log_mass - (mrow + jnp.log(tot)) + quarter_nx
        packed = jnp.where(lanes == PADDED - 1, jnp.broadcast_to(fcol, num.shape), num)
        rows = jnp.transpose(packed)
        f_ref[s] = rows[PADDED - 1 : PADDED, :]
        off = pl.multiple_of(s * bs, bs)
        xcols = x_ref[:, pl.ds(off, bs)].astype(jnp.float32)
        drift_ref[:, pl.ds(off, bs)] = rows[:ncomp] / rows[ncomp : ncomp + 1] - xcols
        return carry

    lax.fori_loop(0, nblk, block, 0)


def _specs(kinds):
    return [pl.BlockSpec(memory_space=pltpu.SMEM if k == "s" else pltpu.VMEM) for k in kinds]


def local(source_coords, target_coords, target_potential, fetch_blocks, pair_slots, pair_counts):
    ncomp = source_coords.shape[0]
    nblk = pair_counts.shape[0]
    bs = source_coords.shape[1] // nblk
    peers = lax.axis_size("blocks")
    cap = fetch_blocks.shape[2]
    nslot = peers * cap
    most = pair_slots.shape[1]
    log_mass = -math.log(peers * nblk * bs)
    chunks = most // CHUNK
    assert most % CHUNK == 0

    wanted = fetch_blocks[0]
    me = lax.axis_index("blocks")
    fetch_all = lax.all_to_all(
        jnp.broadcast_to(wanted[None], (peers, peers, cap)), "blocks", split_axis=0, concat_axis=0, tiled=True
    )
    asked = lax.dynamic_index_in_dim(fetch_all, me, axis=1, keepdims=False)
    asked_local = (asked % nblk).reshape(-1)

    potential_here = target_potential.reshape(nblk, bs)
    high_wide = lax.reduce_precision(potential_here, exponent_bits=8, mantissa_bits=7)
    rest = potential_here - high_wide
    middle_wide = lax.reduce_precision(rest, exponent_bits=8, mantissa_bits=7)
    high = high_wide.astype(jnp.bfloat16)
    middle = middle_wide.astype(jnp.bfloat16)
    low = (rest - middle_wide).astype(jnp.bfloat16)
    target_blocks = jnp.concatenate(
        [jnp.transpose(target_coords.reshape(ncomp, nblk, bs), (1, 0, 2)), high[:, None], middle[:, None], low[:, None]],
        axis=1,
    )
    send = target_blocks[asked_local].reshape(peers, cap, ncomp + 3, bs)
    came = lax.all_to_all(send, "blocks", split_axis=0, concat_axis=0, tiled=True).reshape(nslot, ncomp + 3, bs)
    pieces = came[:, ncomp:, :].astype(jnp.float32)
    slot_potential = (pieces[:, 0:1] + pieces[:, 1:2]) + pieces[:, 2:3]
    came_coords = came[:, :ncomp, :]
    came_wide = came_coords.astype(jnp.float32)
    quarter_ny = 0.25 * jnp.sum(came_wide * came_wide, axis=1, keepdims=True)
    slot_coords = jnp.concatenate(
        [
            came_coords,
            jnp.ones((nslot, 1, bs), jnp.bfloat16),
            jnp.zeros((nslot, PADDED - ncomp - 1, bs), jnp.bfloat16),
        ],
        axis=1,
    )
    slot_rows = jnp.concatenate(
        [jnp.transpose(slot_coords, (0, 2, 1)), jnp.zeros((nslot, bs, bs - PADDED), jnp.bfloat16)], axis=2
    )
    halved = (source_coords.astype(jnp.float32) * 0.5).astype(jnp.bfloat16)
    halved = jnp.concatenate([halved, jnp.zeros((PADDED - ncomp, nblk * bs), jnp.bfloat16)], axis=0)
    source_rows = jnp.transpose(halved.reshape(PADDED, nblk, bs), (1, 2, 0))
    flat_slots = pair_slots.reshape(-1)

    vmem = 48 * 1024 * 1024
    scratch = [pltpu.VMEM((nslot, 1, bs), jnp.float32), pltpu.VMEM((chunks, bs, CHUNK * bs), jnp.float32)]
    sweep = pl.pallas_call(
        functools.partial(sweep_kernel, most=most, log_mass=log_mass),
        out_shape=jax.ShapeDtypeStruct((nslot, 1, bs), jnp.float32),
        in_specs=_specs("ssvvvv"),
        out_specs=_specs("v")[0],
        scratch_shapes=[pltpu.VMEM((nslot, 1, bs), jnp.float32)] * 2 + scratch[1:],
        compiler_params=pltpu.CompilerParams(vmem_limit_bytes=vmem),
    )
    final = pl.pallas_call(
        functools.partial(final_kernel, most=most, log_mass=log_mass, ncomp=ncomp),
        out_shape=(
            jax.ShapeDtypeStruct((nblk, 1, bs), jnp.float32),
            jax.ShapeDtypeStruct((ncomp, nblk * bs), jnp.float32),
        ),
        in_specs=_specs("ssvvvvv"),
        out_specs=tuple(_specs("vv")),
        scratch_shapes=scratch[1:],
        compiler_params=pltpu.CompilerParams(vmem_limit_bytes=vmem),
    )

    def combine(values, match, previous, axes):
        merged = jnp.max(jnp.where(match, values, floor_value), axis=axes)
        summed = jnp.sum(jnp.where(match, jnp.exp(values - jnp.expand_dims(merged, axes)), 0.0), axis=axes)
        reached = merged > 0.5 * floor_value
        return jnp.where(reached, log_mass - (merged + jnp.log(jnp.where(reached, summed, 1.0))), previous)

    owned = (asked_local.reshape(peers, cap)[None] == jnp.arange(nblk, dtype=jnp.int32)[:, None, None])[..., None]
    gather_all = peers * nslot * bs * 4 <= (1 << 20)
    if gather_all:
        fetched = jnp.transpose(fetch_all, (1, 0, 2))[:, None, :, :] == wanted[:, :, None, None]
        fetched = fetched[..., None]
    for sweep_index in range(SWEEPS):
        lse = sweep(
            flat_slots, pair_counts, source_rows, slot_coords, slot_potential - quarter_ny, slot_potential
        ).reshape(nslot, bs)
        if gather_all:
            came = lax.all_to_all(
                jnp.broadcast_to(lse[None], (peers, nslot, bs)), "blocks", split_axis=0, concat_axis=0, tiled=True
            ).reshape(peers, peers, cap, bs)
            mine = lax.dynamic_index_in_dim(came, me, axis=1, keepdims=False)
            potential_here = combine(mine[None], owned, potential_here, (1, 2))
            by_owner = jnp.transpose(came, (1, 0, 2, 3))[:, None]
            slot_potential = combine(
                by_owner, fetched, slot_potential.reshape(peers, cap, bs), (2, 3)
            ).reshape(nslot, 1, bs)
        else:
            came = lax.all_to_all(
                lse.reshape(peers, cap, bs), "blocks", split_axis=0, concat_axis=0, tiled=True
            )
            potential_here = combine(came[None], owned, potential_here, (1, 2))
            send_potential = potential_here[asked_local].reshape(peers, cap, bs)
            slot_potential = lax.all_to_all(
                send_potential, "blocks", split_axis=0, concat_axis=0, tiled=True
            ).reshape(nslot, 1, bs)

    source_side, drift = final(
        flat_slots, pair_counts, source_rows, source_coords, slot_coords, slot_rows, slot_potential - quarter_ny
    )
    return (source_side.reshape(-1), potential_here.reshape(-1), drift)


def solution(mesh):
    return jax.shard_map(
        local,
        mesh=mesh,
        in_specs=(
            P(None, ("groups", "blocks")),
            P(None, ("groups", "blocks")),
            P(("groups", "blocks")),
            P(("groups", "blocks"), None, None),
            P(("groups", "blocks"), None),
            P(("groups", "blocks")),
        ),
        out_specs=(P(("groups", "blocks")), P(("groups", "blocks")), P(None, ("groups", "blocks"))),
        check_vma=False,
    )
```

profile of v0, /device:TPU:1, one launch (start us, length us, event | category | flops | bytes accessed | tf_op | source)
XLA Modules:
  0.0 100.9 jit_solution(12205840718530474724)
XLA Ops:
  0.6 0.0 copy-start.4
  0.6 0.0 copy-start.2
  0.7 0.7 copy-done.4
  1.3 0.6 broadcast_in_dim.147
  1.9 7.3 %all-to-all-start = ((s32[16,16,2]{1,2,0:T(2,128)}), s32[16,16,2]{1,2,0:T(2,128)S(1)}, u32[]{:S(2)}, u32[]{:S(2)}) async-start(s32[16,16,2]{1,2,0:T(2,128)} %broadcast_in_dim.147), calls=%async_computation | async-start | bytes 32768 | tf_op jit(solution)/shard_map/all_to_all | solution.py:153
  9.3 0.7 reduce-precision_convert_fusion.1
  10.0 0.0 copy-done.2
  10.1 5.0 %all-to-all-done = s32[16,16,2]{1,2,0:T(2,128)S(1)} async-done(((s32[16,16,2]{1,2,0:T(2,128)}), s32[16,16,2]{1,2,0:T(2,128)S(1)}, u32[]{:S(2)}, u32[]{:S(2)}) %all-to-all-start) | async-done | bytes 2080 | tf_op jit(solution)/shard_map/all_to_all | solution.py:153
  15.1 0.4 fusion.19
  15.5 0.1 squeeze.9
  15.6 0.6 gather_fusion
  16.3 0.9 copy.84
  17.2 0.0 copy-start
  17.2 4.2 %all-to-all-start.1 = ((bf16[16,2,33,128]{3,1,2,0:T(2,128)(2,1)}), bf16[16,2,33,128]{3,1,2,0:T(2,128)(2,1)S(1)}, u32[]{:S(2)}, u32[]{:S(2)}) async-start(bf16[16,2,33,128]{3,1,2,0:T(2,128)(2,1)} %copy.84), calls=%async_computation.1 | async-start | bytes 540672 | tf_op jit(solution)/shard_map/all_to_all | solution.py:171
  21.4 0.0 copy-start.5
  21.4 0.1 pad.4.clone
  21.5 0.1 pad.3.clone
  21.6 0.5 copy-done.5
  22.1 0.1 reshape.293.slots_ref
  22.2 0.0 copy-done
  22.2 0.2 copy.92
  22.4 0.1 concatenate.12.clone
  22.4 8.7 %all-to-all-done.1 = bf16[16,2,33,128]{3,1,2,0:T(2,128)(2,1)S(1)} async-done(((bf16[16,2,33,128]{3,1,2,0:T(2,128)(2,1)}), bf16[16,2,33,128]{3,1,2,0:T(2,128)(2,1)S(1)}, u32[]{:S(2)}, u32[]{:S(2)}) %all-to-all-start.1) | async-done | bytes 270368 | tf_op jit(solution)/shard_map/all_to_all | solution.py:171
  31.2 0.1 multiply_reduce_fusion
  31.4 0.1 maximum_maximum_fusion.y_ref
  31.5 0.0 copy-start.1
  31.5 0.6 copy-done.1
  32.2 11.8 %shard_map.85 = f32[32,1,128]{2,1,0:T(1,128)S(1)} custom-call(s32[256]{0:T(256)S(1)} %reshape.293.slots_ref, s32[8]{0:T(128)S(1)} %copy-done.1, bf16[8,128,32]{2,1,0:T(8,128)(2,1)S(1)} %bitcast.72, bf16[32,32,128]{2,1,0:T(8,128)(2,1)S(1)} %maximum_maximum_fusion.y_ref, f32[32,1,128]{2,1,0:T(1,128)S(1)} %get-tuple-element.11.h_ref, ...), custom_call_target="tpu_custom_call" | custom-call | tf_op jit(solution)/shard_map/pallas_call | solution.py:227
  44.0 0.7 broadcast_in_dim.152
  44.7 4.3 %all-to-all-start.2 = ((f32[16,32,128]{2,1,0:T(8,128)}), f32[16,32,128]{2,1,0:T(8,128)S(1)}, u32[]{:S(2)}, u32[]{:S(2)}) async-start(f32[16,32,128]{2,1,0:T(8,128)} %broadcast_in_dim.152), calls=%async_computation.2 | async-start | bytes 524288 | tf_op jit(solution)/shard_map/all_to_all | solution.py:231
  49.0 0.1 copy.87
  49.1 0.1 copy.86
  49.2 0.1 copy.91
  49.3 0.1 broadcast_compare_fusion
  49.4 9.2 %all-to-all-done.2 = f32[16,32,128]{2,1,0:T(8,128)S(1)} async-done(((f32[16,32,128]{2,1,0:T(8,128)}), f32[16,32,128]{2,1,0:T(8,128)S(1)}, u32[]{:S(2)}, u32[]{:S(2)}) %all-to-all-start.2) | async-done | bytes 262176 | tf_op jit(solution)/shard_map/all_to_all | solution.py:231
  58.6 0.2 copy.88
  58.7 0.2 select_reduce_fusion.3
  58.9 0.2 select_reduce_fusion.2
  59.2 0.1 fusion.17
  59.3 11.8 %shard_map.86 = f32[32,1,128]{2,1,0:T(1,128)S(1)} custom-call(s32[256]{0:T(256)S(1)} %reshape.293.slots_ref, s32[8]{0:T(128)S(1)} %copy-done.1, bf16[8,128,32]{2,1,0:T(8,128)(2,1)S(1)} %bitcast.73, bf16[32,32,128]{2,1,0:T(8,128)(2,1)S(1)} %maximum_maximum_fusion.y_ref, f32[32,1,128]{2,1,0:T(1,128)S(1)} %get-tuple-element.9.h_ref, ...), custom_call_target="tpu_custom_call" | custom-call | tf_op jit(solution)/shard_map/pallas_call | solution.py:227
  71.1 0.7 broadcast_in_dim.158
  71.8 4.2 %all-to-all-start.3 = ((f32[16,32,128]{2,1,0:T(8,128)}), f32[16,32,128]{2,1,0:T(8,128)S(1)}, u32[]{:S(2)}, u32[]{:S(2)}) async-start(f32[16,32,128]{2,1,0:T(8,128)} %broadcast_in_dim.158), calls=%async_computation.3 | async-start | bytes 524288 | tf_op jit(solution)/shard_map/all_to_all | solution.py:231
  76.1 0.1 fusion.20
  76.2 0.5 copy.93
  76.7 0.3 concatenate.15.clone.yT_ref
  77.0 8.6 %all-to-all-done.3 = f32[16,32,128]{2,1,0:T(8,128)S(1)} async-done(((f32[16,32,128]{2,1,0:T(8,128)}), f32[16,32,128]{2,1,0:T(8,128)S(1)}, u32[]{:S(2)}, u32[]{:S(2)}) %all-to-all-start.3) | async-done | bytes 262176 | tf_op jit(solution)/shard_map/all_to_all | solution.py:231
  85.6 0.2 copy.89
  85.8 0.1 select_reduce_fusion.7
  85.9 0.1 select_reduce_fusion.6
  86.0 0.1 select_reduce_fusion.4
  86.1 0.2 select_reduce_fusion.1
  86.4 0.0 copy-start.3
  86.4 0.2 select_reduce_fusion
  86.6 0.4 copy-done.3
  87.1 0.6 fusion.10
  87.7 0.1 fusion.4.h_ref
  87.7 13.2 %shard_map.87 = (f32[8,1,128]{2,1,0:T(1,128)}, f32[30,1024]{1,0:T(8,128)}) custom-call(s32[256]{0:T(256)S(1)} %reshape.293.slots_ref, s32[8]{0:T(128)S(1)} %copy-done.1, bf16[8,128,32]{2,1,0:T(8,128)(2,1)S(1)} %bitcast.74, bf16[30,1024]{1,0:T(8,128)(2,1)S(1)} %copy-done, bf16[32,32,128]{2,1,0:T(8,128)(2,1)S(1)} %maximum_maximum_fusion.y_ref, ...), custom_call_target="tpu_custom_call" | custom-call | tf_op jit(solution)/shard_map/pallas_call | solution.py:250
  (18 shorter events, 0.3 us)
Async XLA Ops:
  0.6 0.7 copy-start.4
  0.6 9.3 %copy-start.2 = (bf16[30,1024]{1,0:T(8,128)(2,1)S(1)}, bf16[30,1024]{1,0:T(8,128)(2,1)}, u32[]{:S(2)}) copy-start(bf16[30,1024]{1,0:T(8,128)(2,1)} %param.7) | copy-start | bytes 184324
  1.9 13.2 %all-to-all-start = ((s32[16,16,2]{1,2,0:T(2,128)}), s32[16,16,2]{1,2,0:T(2,128)S(1)}, u32[]{:S(2)}, u32[]{:S(2)}) async-start(s32[16,16,2]{1,2,0:T(2,128)} %broadcast_in_dim.147), calls=%async_computation | async-start | bytes 32768 | tf_op jit(solution)/shard_map/all_to_all | solution.py:153
  17.2 5.0 %copy-start = (bf16[30,1024]{1,0:T(8,128)(2,1)S(1)}, bf16[30,1024]{1,0:T(8,128)(2,1)}, u32[]{:S(2)}) copy-start(bf16[30,1024]{1,0:T(8,128)(2,1)} %x_ref.1) | copy-start | bytes 184324
  17.2 13.9 %all-to-all-start.1 = ((bf16[16,2,33,128]{3,1,2,0:T(2,128)(2,1)}), bf16[16,2,33,128]{3,1,2,0:T(2,128)(2,1)S(1)}, u32[]{:S(2)}, u32[]{:S(2)}) async-start(bf16[16,2,33,128]{3,1,2,0:T(2,128)(2,1)} %copy.84), calls=%async_computation.1 | async-start | bytes 540672 | tf_op jit(solution)/shard_map/all_to_all | solution.py:171
  21.4 0.7 copy-start.5
  31.5 0.7 copy-start.1
  44.7 13.8 %all-to-all-start.2 = ((f32[16,32,128]{2,1,0:T(8,128)}), f32[16,32,128]{2,1,0:T(8,128)S(1)}, u32[]{:S(2)}, u32[]{:S(2)}) async-start(f32[16,32,128]{2,1,0:T(8,128)} %broadcast_in_dim.152), calls=%async_computation.2 | async-start | bytes 524288 | tf_op jit(solution)/shard_map/all_to_all | solution.py:231
  71.8 13.8 %all-to-all-start.3 = ((f32[16,32,128]{2,1,0:T(8,128)}), f32[16,32,128]{2,1,0:T(8,128)S(1)}, u32[]{:S(2)}, u32[]{:S(2)}) async-start(f32[16,32,128]{2,1,0:T(8,128)} %broadcast_in_dim.158), calls=%async_computation.3 | async-start | bytes 524288 | tf_op jit(solution)/shard_map/all_to_all | solution.py:231
  86.4 0.7 copy-start.3
where the time goes:
time: 102 us; the launch traced here: 101 us
  Pallas kernels  36.9 us (36%)
  waiting for transfers between devices  31.4 us (31%)
  starting transfers between devices  20.1 us (20%)
  local copies, waits for them, and re-layouts  8.29 us (8%)
  other arithmetic  3.33 us (3%)
    pallas_call x2, Pallas kernels, local(): sweep(flat_slots, pair_counts, source_rows, slot_coords, slot_potential -...  23.7 us
    all_to_all x2, waiting for transfers between devices, local(): lax.all_to_all(jnp.broadcast_to(lse[None], (peers, nslot, bs)), 'blocks',...  17.7 us
    pallas_call x1, Pallas kernels, local(): final(flat_slots, pair_counts, source_rows, source_coords, slot_coords, s...  13.2 us
    all_to_all x1, waiting for transfers between devices, local(): lax.all_to_all(send, 'blocks', split_axis=0, concat_axis=0, tiled=True)  8.69 us
    all_to_all x2, starting transfers between devices, local(): lax.all_to_all(jnp.broadcast_to(lse[None], (peers, nslot, bs)), 'blocks',...  8.53 us
    all_to_all x1, starting transfers between devices, local(): lax.all_to_all(jnp.broadcast_to(wanted[None], (peers, peers, cap)), 'bloc...  7.34 us
    all_to_all x1, waiting for transfers between devices, local(): lax.all_to_all(jnp.broadcast_to(wanted[None], (peers, peers, cap)), 'bloc...  5.01 us
    all_to_all x1, starting transfers between devices, local(): lax.all_to_all(send, 'blocks', split_axis=0, concat_axis=0, tiled=True)  4.21 us
  transfers between devices with their start and end apart: 4, of which 4 were waited for; matrix products, arithmetic and copies ran while one was open for 3% of the time, Pallas kernels for 0%

commit v1 on v0

--- a/solution.py
+++ b/solution.py
@@ -24,16 +24,11 @@
 
 
 def _row_scores(s, cnt, slots_ref, xs, y_ref, h_ref, s_ref, most, bs):
-    lane_tile = lax.broadcasted_iota(jnp.int32, (1, CHUNK * bs), 1) // bs
-
     def first(q, m):
         sls = _chunk_slots(slots_ref, s, q, most)
-        rhs = jnp.concatenate([y_ref[sl] for sl in sls], axis=1)
-        hrow = jnp.concatenate([h_ref[sl] for sl in sls], axis=1)
-        hrow = jnp.where(lane_tile + q * CHUNK < cnt, hrow, floor_value)
-        sc = jnp.dot(xs, rhs, preferred_element_type=jnp.float32) + hrow
-        for t in range(CHUNK):
-            tile = sc[:, t * bs : (t + 1) * bs]
+        for t, sl in enumerate(sls):
+            hrow = jnp.where(q * CHUNK + t < cnt, h_ref[sl], floor_value)
+            tile = jnp.dot(xs, y_ref[sl], preferred_element_type=jnp.float32) + hrow
             s_ref[q, :, t * bs : (t + 1) * bs] = tile
             m = jnp.maximum(m, tile)
         return m
@@ -89,7 +84,9 @@
     lax.fori_loop(0, nblk, block, 0)
 
     am = amax_ref[...]
-    lse_ref[...] = jnp.where(am > 0.5 * floor_value, am + jnp.log(asum_ref[...]), floor_value)
+    lse = jnp.where(am > 0.5 * floor_value, am + jnp.log(asum_ref[...]), floor_value)
+    for d in range(lse_ref.shape[0]):
+        lse_ref[d] = lse
 
 
 def final_kernel(slots_ref, counts_ref, xT_ref, x_ref, y_ref, yT_ref, h_ref, f_ref, drift_ref, s_ref, *, most, log_mass, ncomp):
@@ -192,9 +189,11 @@
 
     vmem = 48 * 1024 * 1024
     scratch = [pltpu.VMEM((nslot, 1, bs), jnp.float32), pltpu.VMEM((chunks, bs, CHUNK * bs), jnp.float32)]
+    gather_all = peers * nslot * bs * 4 <= (1 << 20)
+    copies = peers if gather_all else 1
     sweep = pl.pallas_call(
         functools.partial(sweep_kernel, most=most, log_mass=log_mass),
-        out_shape=jax.ShapeDtypeStruct((nslot, 1, bs), jnp.float32),
+        out_shape=jax.ShapeDtypeStruct((copies, nslot, 1, bs), jnp.float32),
         in_specs=_specs("ssvvvv"),
         out_specs=_specs("v")[0],
         scratch_shapes=[pltpu.VMEM((nslot, 1, bs), jnp.float32)] * 2 + scratch[1:],
@@ -219,18 +218,15 @@
         return jnp.where(reached, log_mass - (merged + jnp.log(jnp.where(reached, summed, 1.0))), previous)
 
     owned = (asked_local.reshape(peers, cap)[None] == jnp.arange(nblk, dtype=jnp.int32)[:, None, None])[..., None]
-    gather_all = peers * nslot * bs * 4 <= (1 << 20)
     if gather_all:
         fetched = jnp.transpose(fetch_all, (1, 0, 2))[:, None, :, :] == wanted[:, :, None, None]
         fetched = fetched[..., None]
     for sweep_index in range(SWEEPS):
         lse = sweep(
             flat_slots, pair_counts, source_rows, slot_coords, slot_potential - quarter_ny, slot_potential
-        ).reshape(nslot, bs)
+        )
         if gather_all:
-            came = lax.all_to_all(
-                jnp.broadcast_to(lse[None], (peers, nslot, bs)), "blocks", split_axis=0, concat_axis=0, tiled=True
-            ).reshape(peers, peers, cap, bs)
+            came = lax.all_to_all(lse, "blocks", split_axis=0, concat_axis=0, tiled=True).reshape(peers, peers, cap, bs)
             mine = lax.dynamic_index_in_dim(came, me, axis=1, keepdims=False)
             potential_here = combine(mine[None], owned, potential_here, (1, 2))
             by_owner = jnp.transpose(came, (1, 0, 2, 3))[:, None]

time: 102 us -> 103 us (level)
  the two profiles are of different devices: /device:TPU:1 before, /device:TPU:2 now
where the time goes in v1:
time: 103 us
  Pallas kernels  40.4 us (39%)
  waiting for transfers between devices  33.4 us (32%)
  starting transfers between devices  17.8 us (17%)
  local copies, waits for them, and re-layouts  6.88 us (7%)
  other arithmetic  3.34 us (3%)
    pallas_call x2, Pallas kernels, local(): sweep(flat_slots, pair_counts, source_rows, slot_coords, slot_potential -...  26.6 us
    all_to_all x2, waiting for transfers between devices, local(): lax.all_to_all(lse, 'blocks', split_axis=0, concat_axis=0, tiled=True)  18.7 us
    pallas_call x1, Pallas kernels, local(): final(flat_slots, pair_counts, source_rows, source_coords, slot_coords, s...  13.8 us
    all_to_all x1, waiting for transfers between devices, local(): lax.all_to_all(send, 'blocks', split_axis=0, concat_axis=0, tiled=True)  9.07 us
    all_to_all x2, starting transfers between devices, local(): lax.all_to_all(lse, 'blocks', split_axis=0, concat_axis=0, tiled=True)  8.15 us
    all_to_all x1, starting transfers between devices, local(): lax.all_to_all(jnp.broadcast_to(wanted[None], (peers, peers, cap)), 'bloc...  5.94 us
    all_to_all x1, waiting for transfers between devices, local(): lax.all_to_all(jnp.broadcast_to(wanted[None], (peers, peers, cap)), 'bloc...  5.66 us
    all_to_all x1, starting transfers between devices, local(): lax.all_to_all(send, 'blocks', split_axis=0, concat_axis=0, tiled=True)  3.66 us
  transfers between devices with their start and end apart: 4, of which 4 were waited for; matrix products, arithmetic and copies ran while one was open for 2% of the time, Pallas kernels for 0%

profile of v1, /device:TPU:2, one launch (start us, length us, event | category | flops | bytes accessed | tf_op | source)
XLA Modules:
  0.0 102.8 jit_solution(6657464207445049991)
XLA Ops:
  0.6 0.0 copy-start.4
  0.6 0.0 copy-start.2
  0.7 0.7 copy-done.4
  1.3 0.6 broadcast_in_dim.133
  1.9 5.9 %all-to-all-start = ((s32[16,16,2]{1,2,0:T(2,128)}), s32[16,16,2]{1,2,0:T(2,128)S(1)}, u32[]{:S(2)}, u32[]{:S(2)}) async-start(s32[16,16,2]{1,2,0:T(2,128)} %broadcast_in_dim.133), calls=%async_computation | async-start | bytes 32768 | tf_op jit(solution)/shard_map/all_to_all | solution.py:150
  7.9 0.7 reduce-precision_convert_fusion.1
  8.6 0.0 copy-done.2
  8.7 5.7 %all-to-all-done = s32[16,16,2]{1,2,0:T(2,128)S(1)} async-done(((s32[16,16,2]{1,2,0:T(2,128)}), s32[16,16,2]{1,2,0:T(2,128)S(1)}, u32[]{:S(2)}, u32[]{:S(2)}) %all-to-all-start) | async-done | bytes 2080 | tf_op jit(solution)/shard_map/all_to_all | solution.py:150
  14.4 0.4 fusion.19
  14.8 0.1 squeeze.9
  14.9 0.6 gather_fusion
  15.5 0.9 copy.88
  16.5 0.0 copy-start
  16.5 3.7 %all-to-all-start.1 = ((bf16[16,2,33,128]{3,1,2,0:T(2,128)(2,1)}), bf16[16,2,33,128]{3,1,2,0:T(2,128)(2,1)S(1)}, u32[]{:S(2)}, u32[]{:S(2)}) async-start(bf16[16,2,33,128]{3,1,2,0:T(2,128)(2,1)} %copy.88), calls=%async_computation.1 | async-start | bytes 540672 | tf_op jit(solution)/shard_map/all_to_all | solution.py:168
  20.1 0.0 copy-start.5
  20.1 0.1 pad.4.clone
  20.2 0.1 pad.3.clone
  20.3 0.5 copy-done.5
  20.8 0.1 reshape.291.slots_ref
  20.9 0.0 copy-done
  20.9 0.2 copy.100
  21.1 0.1 concatenate.12.clone
  21.2 9.1 %all-to-all-done.1 = bf16[16,2,33,128]{3,1,2,0:T(2,128)(2,1)S(1)} async-done(((bf16[16,2,33,128]{3,1,2,0:T(2,128)(2,1)}), bf16[16,2,33,128]{3,1,2,0:T(2,128)(2,1)S(1)}, u32[]{:S(2)}, u32[]{:S(2)}) %all-to-all-start.1) | async-done | bytes 270368 | tf_op jit(solution)/shard_map/all_to_all | solution.py:168
  30.3 0.1 multiply_reduce_fusion
  30.5 0.1 maximum_maximum_fusion.y_ref
  30.6 0.0 copy-start.1
  30.6 0.6 copy-done.1
  31.3 13.3 %shard_map.85 = f32[16,32,1,128]{3,2,1,0:T(1,128)} custom-call(s32[256]{0:T(256)S(1)} %reshape.291.slots_ref, s32[8]{0:T(128)S(1)} %copy-done.1, bf16[8,128,32]{2,1,0:T(8,128)(2,1)S(1)} %bitcast.70, bf16[32,32,128]{2,1,0:T(8,128)(2,1)S(1)} %maximum_maximum_fusion.y_ref, f32[32,1,128]{2,1,0:T(1,128)S(1)} %get-tuple-element.11.h_ref, ...), custom_call_target="tpu_custom_call" | custom-call | tf_op jit(solution)/shard_map/pallas_call | solution.py:225
  44.6 4.1 %all-to-all-start.2 = ((f32[16,32,1,128]{3,2,1,0:T(1,128)}), f32[16,32,1,128]{3,2,1,0:T(1,128)S(1)}, u32[]{:S(2)}, u32[]{:S(2)}) async-start(f32[16,32,1,128]{3,2,1,0:T(1,128)} %shard_map.85), calls=%async_computation.2 | async-start | bytes 524288 | tf_op jit(solution)/shard_map/all_to_all | solution.py:229
  48.7 0.1 copy.91
  48.7 0.1 copy.90
  48.8 0.1 copy.95
  48.9 0.1 broadcast_compare_fusion
  49.0 9.6 %all-to-all-done.2 = f32[16,32,1,128]{3,2,1,0:T(1,128)S(1)} async-done(((f32[16,32,1,128]{3,2,1,0:T(1,128)}), f32[16,32,1,128]{3,2,1,0:T(1,128)S(1)}, u32[]{:S(2)}, u32[]{:S(2)}) %all-to-all-start.2) | async-done | bytes 262176 | tf_op jit(solution)/shard_map/all_to_all | solution.py:229
  58.7 0.2 copy.92
  58.8 0.2 select_reduce_fusion.3
  59.1 0.3 select_reduce_fusion.2
  59.3 0.1 fusion.17
  59.4 13.3 %shard_map.86 = f32[16,32,1,128]{3,2,1,0:T(1,128)} custom-call(s32[256]{0:T(256)S(1)} %reshape.291.slots_ref, s32[8]{0:T(128)S(1)} %copy-done.1, bf16[8,128,32]{2,1,0:T(8,128)(2,1)S(1)} %bitcast.71, bf16[32,32,128]{2,1,0:T(8,128)(2,1)S(1)} %maximum_maximum_fusion.y_ref, f32[32,1,128]{2,1,0:T(1,128)S(1)} %get-tuple-element.9.h_ref, ...), custom_call_target="tpu_custom_call" | custom-call | tf_op jit(solution)/shard_map/pallas_call | solution.py:225
  72.7 4.1 %all-to-all-start.3 = ((f32[16,32,1,128]{3,2,1,0:T(1,128)}), f32[16,32,1,128]{3,2,1,0:T(1,128)S(1)}, u32[]{:S(2)}, u32[]{:S(2)}) async-start(f32[16,32,1,128]{3,2,1,0:T(1,128)} %shard_map.86), calls=%async_computation.3 | async-start | bytes 524288 | tf_op jit(solution)/shard_map/all_to_all | solution.py:229
  76.8 0.1 fusion.20
  76.9 0.5 copy.101
  77.4 0.3 concatenate.15.clone.yT_ref
  77.7 9.1 %all-to-all-done.3 = f32[16,32,1,128]{3,2,1,0:T(1,128)S(1)} async-done(((f32[16,32,1,128]{3,2,1,0:T(1,128)}), f32[16,32,1,128]{3,2,1,0:T(1,128)S(1)}, u32[]{:S(2)}, u32[]{:S(2)}) %all-to-all-start.3) | async-done | bytes 262176 | tf_op jit(solution)/shard_map/all_to_all | solution.py:229
  86.8 0.1 select_reduce_fusion.7
  86.9 0.1 select_reduce_fusion.6
  87.0 0.1 select_reduce_fusion.4
  87.2 0.2 copy.93
  87.3 0.2 select_reduce_fusion.1
  87.6 0.0 copy-start.3
  87.6 0.3 select_reduce_fusion
  87.8 0.4 copy-done.3
  88.3 0.6 fusion.10
  88.9 0.1 fusion.4.h_ref
  88.9 13.8 %shard_map.87 = (f32[8,1,128]{2,1,0:T(1,128)}, f32[30,1024]{1,0:T(8,128)}) custom-call(s32[256]{0:T(256)S(1)} %reshape.291.slots_ref, s32[8]{0:T(128)S(1)} %copy-done.1, bf16[8,128,32]{2,1,0:T(8,128)(2,1)S(1)} %bitcast.72, bf16[30,1024]{1,0:T(8,128)(2,1)S(1)} %copy-done, bf16[32,32,128]{2,1,0:T(8,128)(2,1)S(1)} %maximum_maximum_fusion.y_ref, ...), custom_call_target="tpu_custom_call" | custom-call | tf_op jit(solution)/shard_map/pallas_call | solution.py:246
  (20 shorter events, 0.3 us)
Async XLA Ops:
  0.6 0.7 copy-start.4
  0.6 8.0 %copy-start.2 = (bf16[30,1024]{1,0:T(8,128)(2,1)S(1)}, bf16[30,1024]{1,0:T(8,128)(2,1)}, u32[]{:S(2)}) copy-start(bf16[30,1024]{1,0:T(8,128)(2,1)} %param.7) | copy-start | bytes 184324
  1.9 12.4 %all-to-all-start = ((s32[16,16,2]{1,2,0:T(2,128)}), s32[16,16,2]{1,2,0:T(2,128)S(1)}, u32[]{:S(2)}, u32[]{:S(2)}) async-start(s32[16,16,2]{1,2,0:T(2,128)} %broadcast_in_dim.133), calls=%async_computation | async-start | bytes 32768 | tf_op jit(solution)/shard_map/all_to_all | solution.py:150
  16.5 4.4 %copy-start = (bf16[30,1024]{1,0:T(8,128)(2,1)S(1)}, bf16[30,1024]{1,0:T(8,128)(2,1)}, u32[]{:S(2)}) copy-start(bf16[30,1024]{1,0:T(8,128)(2,1)} %x_ref.1) | copy-start | bytes 184324
  16.5 13.8 %all-to-all-start.1 = ((bf16[16,2,33,128]{3,1,2,0:T(2,128)(2,1)}), bf16[16,2,33,128]{3,1,2,0:T(2,128)(2,1)S(1)}, u32[]{:S(2)}, u32[]{:S(2)}) async-start(bf16[16,2,33,128]{3,1,2,0:T(2,128)(2,1)} %copy.88), calls=%async_computation.1 | async-start | bytes 540672 | tf_op jit(solution)/shard_map/all_to_all | solution.py:168
  20.1 0.7 copy-start.5
  30.6 0.7 copy-start.1
  44.6 14.1 %all-to-all-start.2 = ((f32[16,32,1,128]{3,2,1,0:T(1,128)}), f32[16,32,1,128]{3,2,1,0:T(1,128)S(1)}, u32[]{:S(2)}, u32[]{:S(2)}) async-start(f32[16,32,1,128]{3,2,1,0:T(1,128)} %shard_map.85), calls=%async_computation.2 | async-start | bytes 524288 | tf_op jit(solution)/shard_map/all_to_all | solution.py:229
  72.7 14.1 %all-to-all-start.3 = ((f32[16,32,1,128]{3,2,1,0:T(1,128)}), f32[16,32,1,128]{3,2,1,0:T(1,128)S(1)}, u32[]{:S(2)}, u32[]{:S(2)}) async-start(f32[16,32,1,128]{3,2,1,0:T(1,128)} %shard_map.86), calls=%async_computation.3 | async-start | bytes 524288 | tf_op jit(solution)/shard_map/all_to_all | solution.py:229
  87.6 0.7 copy-start.3

commit v2 on v1

--- a/solution.py
+++ b/solution.py
@@ -13,6 +13,8 @@
 floor_value = -1e30
 PADDED = 32
 CHUNK = 8
+LOG2E = 1.4426950408889634
+LN2 = 0.6931471805599453
 
 
 def _chunk_slots(slots_ref, s, q, most):
@@ -28,7 +30,7 @@
         sls = _chunk_slots(slots_ref, s, q, most)
         for t, sl in enumerate(sls):
             hrow = jnp.where(q * CHUNK + t < cnt, h_ref[sl], floor_value)
-            tile = jnp.dot(xs, y_ref[sl], preferred_element_type=jnp.float32) + hrow
+            tile = (jnp.dot(xs, y_ref[sl], preferred_element_type=jnp.float32) + hrow) * LOG2E
             s_ref[q, :, t * bs : (t + 1) * bs] = tile
             m = jnp.maximum(m, tile)
         return m
@@ -51,12 +53,12 @@
 
         def second(q, acc):
             for t in range(CHUNK):
-                acc = acc + jnp.exp(s_ref[q, :, t * bs : (t + 1) * bs] - mb)
+                acc = acc + jnp.exp2(s_ref[q, :, t * bs : (t + 1) * bs] - mb)
             return acc
 
         acc = lax.fori_loop(0, nq, second, jnp.zeros((bs, bs), jnp.float32))
         tot = jnp.sum(acc, axis=1, keepdims=True)
-        kb = jnp.broadcast_to(log_mass - (mrow + jnp.log(tot)), (bs, bs))
+        kb = jnp.broadcast_to((log_mass - (mrow * LN2 + jnp.log(tot))) * LOG2E, (bs, bs))
 
         def column(q, c):
             sls = _chunk_slots(slots_ref, s, q, most)
@@ -65,9 +67,9 @@
                 v = s_ref[q, :, t * bs : (t + 1) * bs] + kb
                 cm = jnp.max(v, axis=0, keepdims=True)
                 cms.append(cm)
-                ces.append(jnp.sum(jnp.exp(v - cm), axis=0, keepdims=True))
+                ces.append(jnp.sum(jnp.exp2(v - cm), axis=0, keepdims=True))
             valid = tile_row + q * CHUNK < cnt
-            tm = jnp.where(valid, _rows_of(cms) - _rows_of([g_ref[sl] for sl in sls]), floor_value)
+            tm = jnp.where(valid, _rows_of(cms) * LN2 - _rows_of([g_ref[sl] for sl in sls]), floor_value)
             te = jnp.where(valid, _rows_of(ces), 0.0)
             om = _rows_of([amax_ref[sl] for sl in sls])
             os = _rows_of([asum_ref[sl] for sl in sls])
@@ -103,7 +105,7 @@
             acc, num = c
             sls = _chunk_slots(slots_ref, s, q, most)
             for t, sl in enumerate(sls):
-                e = jnp.exp(s_ref[q, :, t * bs : (t + 1) * bs] - mb)
+                e = jnp.exp2(s_ref[q, :, t * bs : (t + 1) * bs] - mb)
                 acc = acc + e
                 num = num + jnp.dot(e.astype(jnp.bfloat16), yT_ref[sl], preferred_element_type=jnp.float32)
             return acc, num
@@ -117,7 +119,7 @@
         tot = jnp.sum(acc, axis=1, keepdims=True)
         xf = xs.astype(jnp.float32)
         quarter_nx = jnp.sum(xf * xf, axis=1, keepdims=True)
-        fcol = log_mass - (mrow + jnp.log(tot)) + quarter_nx
+        fcol = log_mass - (mrow * LN2 + jnp.log(tot)) + quarter_nx
         packed = jnp.where(lanes == PADDED - 1, jnp.broadcast_to(fcol, num.shape), num)
         rows = jnp.transpose(packed)
         f_ref[s] = rows[PADDED - 1 : PADDED, :]

time: 103 us -> 105 us (1.019)
  the two profiles are of different devices: /device:TPU:2 before, /device:TPU:0 now
where the time goes in v2:
time: 105 us; the launch traced here: 106 us
  Pallas kernels  42.9 us (41%)
  waiting for transfers between devices  33.3 us (32%)
  starting transfers between devices  18.1 us (17%)
  local copies, waits for them, and re-layouts  6.88 us (7%)
  other arithmetic  3.34 us (3%)
    pallas_call x2, Pallas kernels, local(): sweep(flat_slots, pair_counts, source_rows, slot_coords, slot_potential -...  28.3 us
    all_to_all x2, waiting for transfers between devices, local(): lax.all_to_all(lse, 'blocks', split_axis=0, concat_axis=0, tiled=True)  18.6 us
    pallas_call x1, Pallas kernels, local(): final(flat_slots, pair_counts, source_rows, source_coords, slot_coords, s...  14.6 us
    all_to_all x1, waiting for transfers between devices, local(): lax.all_to_all(send, 'blocks', split_axis=0, concat_axis=0, tiled=True)  9.07 us
    all_to_all x1, starting transfers between devices, local(): lax.all_to_all(jnp.broadcast_to(wanted[None], (peers, peers, cap)), 'bloc...  7.41 us
    all_to_all x2, starting transfers between devices, local(): lax.all_to_all(lse, 'blocks', split_axis=0, concat_axis=0, tiled=True)  7.06 us
    all_to_all x1, waiting for transfers between devices, local(): lax.all_to_all(jnp.broadcast_to(wanted[None], (peers, peers, cap)), 'bloc...  5.66 us
    all_to_all x1, starting transfers between devices, local(): lax.all_to_all(send, 'blocks', split_axis=0, concat_axis=0, tiled=True)  3.66 us
  transfers between devices with their start and end apart: 4, of which 4 were waited for; matrix products, arithmetic and copies ran while one was open for 2% of the time, Pallas kernels for 0%

profile of v2, /device:TPU:0, one launch (start us, length us, event | category | flops | bytes accessed | tf_op | source)
XLA Modules:
  0.0 105.5 jit_solution(11614751559204872588)
XLA Ops:
  0.6 0.0 copy-start.4
  0.6 0.0 copy-start.2
  0.7 0.7 copy-done.4
  1.3 0.6 broadcast_in_dim.133
  1.9 7.4 %all-to-all-start = ((s32[16,16,2]{1,2,0:T(2,128)}), s32[16,16,2]{1,2,0:T(2,128)S(1)}, u32[]{:S(2)}, u32[]{:S(2)}) async-start(s32[16,16,2]{1,2,0:T(2,128)} %broadcast_in_dim.133), calls=%async_computation | async-start | bytes 32768 | tf_op jit(solution)/shard_map/all_to_all | solution.py:152
  9.3 0.7 reduce-precision_convert_fusion.1
  10.1 0.0 copy-done.2
  10.2 5.7 %all-to-all-done = s32[16,16,2]{1,2,0:T(2,128)S(1)} async-done(((s32[16,16,2]{1,2,0:T(2,128)}), s32[16,16,2]{1,2,0:T(2,128)S(1)}, u32[]{:S(2)}, u32[]{:S(2)}) %all-to-all-start) | async-done | bytes 2080 | tf_op jit(solution)/shard_map/all_to_all | solution.py:152
  15.8 0.4 fusion.19
  16.3 0.1 squeeze.9
  16.4 0.6 gather_fusion
  17.0 0.9 copy.88
  17.9 0.0 copy-start
  17.9 3.7 %all-to-all-start.1 = ((bf16[16,2,33,128]{3,1,2,0:T(2,128)(2,1)}), bf16[16,2,33,128]{3,1,2,0:T(2,128)(2,1)S(1)}, u32[]{:S(2)}, u32[]{:S(2)}) async-start(bf16[16,2,33,128]{3,1,2,0:T(2,128)(2,1)} %copy.88), calls=%async_computation.1 | async-start | bytes 540672 | tf_op jit(solution)/shard_map/all_to_all | solution.py:170
  21.6 0.0 copy-start.5
  21.6 0.1 pad.4.clone
  21.7 0.1 pad.3.clone
  21.8 0.5 copy-done.5
  22.3 0.1 reshape.291.slots_ref
  22.4 0.0 copy-done
  22.4 0.2 copy.100
  22.6 0.1 concatenate.12.clone
  22.6 9.1 %all-to-all-done.1 = bf16[16,2,33,128]{3,1,2,0:T(2,128)(2,1)S(1)} async-done(((bf16[16,2,33,128]{3,1,2,0:T(2,128)(2,1)}), bf16[16,2,33,128]{3,1,2,0:T(2,128)(2,1)S(1)}, u32[]{:S(2)}, u32[]{:S(2)}) %all-to-all-start.1) | async-done | bytes 270368 | tf_op jit(solution)/shard_map/all_to_all | solution.py:170
  31.8 0.1 multiply_reduce_fusion
  32.0 0.1 maximum_maximum_fusion.y_ref
  32.1 0.0 copy-start.1
  32.1 0.6 copy-done.1
  32.8 14.1 %shard_map.85 = f32[16,32,1,128]{3,2,1,0:T(1,128)} custom-call(s32[256]{0:T(256)S(1)} %reshape.291.slots_ref, s32[8]{0:T(128)S(1)} %copy-done.1, bf16[8,128,32]{2,1,0:T(8,128)(2,1)S(1)} %bitcast.70, bf16[32,32,128]{2,1,0:T(8,128)(2,1)S(1)} %maximum_maximum_fusion.y_ref, f32[32,1,128]{2,1,0:T(1,128)S(1)} %get-tuple-element.11.h_ref, ...), custom_call_target="tpu_custom_call" | custom-call | tf_op jit(solution)/shard_map/pallas_call | solution.py:227
  46.9 3.5 %all-to-all-start.2 = ((f32[16,32,1,128]{3,2,1,0:T(1,128)}), f32[16,32,1,128]{3,2,1,0:T(1,128)S(1)}, u32[]{:S(2)}, u32[]{:S(2)}) async-start(f32[16,32,1,128]{3,2,1,0:T(1,128)} %shard_map.85), calls=%async_computation.2 | async-start | bytes 524288 | tf_op jit(solution)/shard_map/all_to_all | solution.py:231
  50.4 0.1 copy.91
  50.5 0.1 copy.90
  50.6 0.1 copy.95
  50.7 0.1 broadcast_compare_fusion
  50.8 9.6 %all-to-all-done.2 = f32[16,32,1,128]{3,2,1,0:T(1,128)S(1)} async-done(((f32[16,32,1,128]{3,2,1,0:T(1,128)}), f32[16,32,1,128]{3,2,1,0:T(1,128)S(1)}, u32[]{:S(2)}, u32[]{:S(2)}) %all-to-all-start.2) | async-done | bytes 262176 | tf_op jit(solution)/shard_map/all_to_all | solution.py:231
  60.4 0.2 copy.92
  60.6 0.2 select_reduce_fusion.3
  60.8 0.3 select_reduce_fusion.2
  61.1 0.1 fusion.17
  61.1 14.2 %shard_map.86 = f32[16,32,1,128]{3,2,1,0:T(1,128)} custom-call(s32[256]{0:T(256)S(1)} %reshape.291.slots_ref, s32[8]{0:T(128)S(1)} %copy-done.1, bf16[8,128,32]{2,1,0:T(8,128)(2,1)S(1)} %bitcast.71, bf16[32,32,128]{2,1,0:T(8,128)(2,1)S(1)} %maximum_maximum_fusion.y_ref, f32[32,1,128]{2,1,0:T(1,128)S(1)} %get-tuple-element.9.h_ref, ...), custom_call_target="tpu_custom_call" | custom-call | tf_op jit(solution)/shard_map/pallas_call | solution.py:227
  75.3 3.5 %all-to-all-start.3 = ((f32[16,32,1,128]{3,2,1,0:T(1,128)}), f32[16,32,1,128]{3,2,1,0:T(1,128)S(1)}, u32[]{:S(2)}, u32[]{:S(2)}) async-start(f32[16,32,1,128]{3,2,1,0:T(1,128)} %shard_map.86), calls=%async_computation.3 | async-start | bytes 524288 | tf_op jit(solution)/shard_map/all_to_all | solution.py:231
  78.8 0.1 fusion.20
  79.0 0.5 copy.101
  79.5 0.3 concatenate.15.clone.yT_ref
  79.8 9.0 %all-to-all-done.3 = f32[16,32,1,128]{3,2,1,0:T(1,128)S(1)} async-done(((f32[16,32,1,128]{3,2,1,0:T(1,128)}), f32[16,32,1,128]{3,2,1,0:T(1,128)S(1)}, u32[]{:S(2)}, u32[]{:S(2)}) %all-to-all-start.3) | async-done | bytes 262176 | tf_op jit(solution)/shard_map/all_to_all | solution.py:231
  88.8 0.1 select_reduce_fusion.7
  89.0 0.1 select_reduce_fusion.6
  89.1 0.1 select_reduce_fusion.4
  89.2 0.2 copy.93
  89.4 0.2 select_reduce_fusion.1
  89.6 0.0 copy-start.3
  89.6 0.3 select_reduce_fusion
  89.9 0.4 copy-done.3
  90.3 0.6 fusion.10
  90.9 0.1 fusion.4.h_ref
  90.9 14.6 %shard_map.87 = (f32[8,1,128]{2,1,0:T(1,128)}, f32[30,1024]{1,0:T(8,128)}) custom-call(s32[256]{0:T(256)S(1)} %reshape.291.slots_ref, s32[8]{0:T(128)S(1)} %copy-done.1, bf16[8,128,32]{2,1,0:T(8,128)(2,1)S(1)} %bitcast.72, bf16[30,1024]{1,0:T(8,128)(2,1)S(1)} %copy-done, bf16[32,32,128]{2,1,0:T(8,128)(2,1)S(1)} %maximum_maximum_fusion.y_ref, ...), custom_call_target="tpu_custom_call" | custom-call | tf_op jit(solution)/shard_map/pallas_call | solution.py:248
  (20 shorter events, 0.3 us)
Async XLA Ops:
  0.6 0.7 copy-start.4
  0.6 9.4 %copy-start.2 = (bf16[30,1024]{1,0:T(8,128)(2,1)S(1)}, bf16[30,1024]{1,0:T(8,128)(2,1)}, u32[]{:S(2)}) copy-start(bf16[30,1024]{1,0:T(8,128)(2,1)} %param.7) | copy-start | bytes 184324
  1.9 13.9 %all-to-all-start = ((s32[16,16,2]{1,2,0:T(2,128)}), s32[16,16,2]{1,2,0:T(2,128)S(1)}, u32[]{:S(2)}, u32[]{:S(2)}) async-start(s32[16,16,2]{1,2,0:T(2,128)} %broadcast_in_dim.133), calls=%async_computation | async-start | bytes 32768 | tf_op jit(solution)/shard_map/all_to_all | solution.py:152
  17.9 4.4 %copy-start = (bf16[30,1024]{1,0:T(8,128)(2,1)S(1)}, bf16[30,1024]{1,0:T(8,128)(2,1)}, u32[]{:S(2)}) copy-start(bf16[30,1024]{1,0:T(8,128)(2,1)} %x_ref.1) | copy-start | bytes 184324
  17.9 13.8 %all-to-all-start.1 = ((bf16[16,2,33,128]{3,1,2,0:T(2,128)(2,1)}), bf16[16,2,33,128]{3,1,2,0:T(2,128)(2,1)S(1)}, u32[]{:S(2)}, u32[]{:S(2)}) async-start(bf16[16,2,33,128]{3,1,2,0:T(2,128)(2,1)} %copy.88), calls=%async_computation.1 | async-start | bytes 540672 | tf_op jit(solution)/shard_map/all_to_all | solution.py:170
  21.6 0.7 copy-start.5
  32.1 0.7 copy-start.1
  46.9 13.5 %all-to-all-start.2 = ((f32[16,32,1,128]{3,2,1,0:T(1,128)}), f32[16,32,1,128]{3,2,1,0:T(1,128)S(1)}, u32[]{:S(2)}, u32[]{:S(2)}) async-start(f32[16,32,1,128]{3,2,1,0:T(1,128)} %shard_map.85), calls=%async_computation.2 | async-start | bytes 524288 | tf_op jit(solution)/shard_map/all_to_all | solution.py:231
  75.3 13.5 %all-to-all-start.3 = ((f32[16,32,1,128]{3,2,1,0:T(1,128)}), f32[16,32,1,128]{3,2,1,0:T(1,128)S(1)}, u32[]{:S(2)}, u32[]{:S(2)}) async-start(f32[16,32,1,128]{3,2,1,0:T(1,128)} %shard_map.86), calls=%async_computation.3 | async-start | bytes 524288 | tf_op jit(solution)/shard_map/all_to_all | solution.py:231
  89.6 0.7 copy-start.3

commit v3 on v2

--- a/solution.py
+++ b/solution.py
@@ -13,12 +13,20 @@
 floor_value = -1e30
 PADDED = 32
 CHUNK = 8
+TAIL = 2
 LOG2E = 1.4426950408889634
 LN2 = 0.6931471805599453
 
 
-def _chunk_slots(slots_ref, s, q, most):
-    return [slots_ref[s * most + jnp.minimum(q * CHUNK + c, most - 1)] for c in range(CHUNK)]
+def _pair_loop(cnt, body, carry):
+    full = cnt // CHUNK
+    carry = lax.fori_loop(0, full, lambda q, c: body(q * CHUNK, CHUNK, c), carry)
+    rest = (cnt - full * CHUNK + TAIL - 1) // TAIL
+    return lax.fori_loop(0, rest, lambda q, c: body(full * CHUNK + q * TAIL, TAIL, c), carry)
+
+
+def _slots_at(slots_ref, s, p0, size, most):
+    return [slots_ref[s * most + p0 + t] for t in range(size)]
 
 
 def _rows_of(values):
@@ -26,49 +34,46 @@
 
 
 def _row_scores(s, cnt, slots_ref, xs, y_ref, h_ref, s_ref, most, bs):
-    def first(q, m):
-        sls = _chunk_slots(slots_ref, s, q, most)
-        for t, sl in enumerate(sls):
-            hrow = jnp.where(q * CHUNK + t < cnt, h_ref[sl], floor_value)
+    def first(p0, size, m):
+        for t, sl in enumerate(_slots_at(slots_ref, s, p0, size, most)):
+            hrow = jnp.where(p0 + t < cnt, h_ref[sl], floor_value)
             tile = (jnp.dot(xs, y_ref[sl], preferred_element_type=jnp.float32) + hrow) * LOG2E
-            s_ref[q, :, t * bs : (t + 1) * bs] = tile
+            s_ref[p0 + t] = tile
             m = jnp.maximum(m, tile)
         return m
 
-    nq = (cnt + CHUNK - 1) // CHUNK
-    m = lax.fori_loop(0, nq, first, jnp.full((bs, bs), floor_value, jnp.float32))
-    return nq, jnp.max(m, axis=1, keepdims=True)
+    m = _pair_loop(cnt, first, jnp.full((bs, bs), floor_value, jnp.float32))
+    return jnp.max(m, axis=1, keepdims=True)
 
 
 def sweep_kernel(slots_ref, counts_ref, xT_ref, y_ref, h_ref, g_ref, lse_ref, amax_ref, asum_ref, s_ref, *, most, log_mass):
     nblk, bs = xT_ref.shape[0], xT_ref.shape[1]
     amax_ref[...] = jnp.full(amax_ref.shape, floor_value, jnp.float32)
     asum_ref[...] = jnp.zeros(asum_ref.shape, jnp.float32)
-    tile_row = lax.broadcasted_iota(jnp.int32, (CHUNK, bs), 0)
 
     def block(s, carry):
         cnt = counts_ref[s]
-        nq, mrow = _row_scores(s, cnt, slots_ref, xT_ref[s], y_ref, h_ref, s_ref, most, bs)
+        mrow = _row_scores(s, cnt, slots_ref, xT_ref[s], y_ref, h_ref, s_ref, most, bs)
         mb = jnp.broadcast_to(mrow, (bs, bs))
 
-        def second(q, acc):
-            for t in range(CHUNK):
-                acc = acc + jnp.exp2(s_ref[q, :, t * bs : (t + 1) * bs] - mb)
+        def second(p0, size, acc):
+            for t in range(size):
+                acc = acc + jnp.exp2(s_ref[p0 + t] - mb)
             return acc
 
-        acc = lax.fori_loop(0, nq, second, jnp.zeros((bs, bs), jnp.float32))
+        acc = _pair_loop(cnt, second, jnp.zeros((bs, bs), jnp.float32))
         tot = jnp.sum(acc, axis=1, keepdims=True)
         kb = jnp.broadcast_to((log_mass - (mrow * LN2 + jnp.log(tot))) * LOG2E, (bs, bs))
 
-        def column(q, c):
-            sls = _chunk_slots(slots_ref, s, q, most)
+        def column(p0, size, c):
+            sls = _slots_at(slots_ref, s, p0, size, most)
             cms, ces = [], []
-            for t in range(CHUNK):
-                v = s_ref[q, :, t * bs : (t + 1) * bs] + kb
+            for t in range(size):
+                v = s_ref[p0 + t] + kb
                 cm = jnp.max(v, axis=0, keepdims=True)
                 cms.append(cm)
                 ces.append(jnp.sum(jnp.exp2(v - cm), axis=0, keepdims=True))
-            valid = tile_row + q * CHUNK < cnt
+            valid = lax.broadcasted_iota(jnp.int32, (size, bs), 0) + p0 < cnt
             tm = jnp.where(valid, _rows_of(cms) * LN2 - _rows_of([g_ref[sl] for sl in sls]), floor_value)
             te = jnp.where(valid, _rows_of(ces), 0.0)
             om = _rows_of([amax_ref[sl] for sl in sls])
@@ -80,7 +85,7 @@
                 asum_ref[sl] = ns[t : t + 1]
             return c
 
-        lax.fori_loop(0, nq, column, 0)
+        _pair_loop(cnt, column, 0)
         return carry
 
     lax.fori_loop(0, nblk, block, 0)
@@ -98,23 +103,19 @@
     def block(s, carry):
         cnt = counts_ref[s]
         xs = xT_ref[s]
-        nq, mrow = _row_scores(s, cnt, slots_ref, xs, y_ref, h_ref, s_ref, most, bs)
+        mrow = _row_scores(s, cnt, slots_ref, xs, y_ref, h_ref, s_ref, most, bs)
         mb = jnp.broadcast_to(mrow, (bs, bs))
 
-        def second(q, c):
+        def second(p0, size, c):
             acc, num = c
-            sls = _chunk_slots(slots_ref, s, q, most)
-            for t, sl in enumerate(sls):
-                e = jnp.exp2(s_ref[q, :, t * bs : (t + 1) * bs] - mb)
+            for t, sl in enumerate(_slots_at(slots_ref, s, p0, size, most)):
+                e = jnp.exp2(s_ref[p0 + t] - mb)
                 acc = acc + e
                 num = num + jnp.dot(e.astype(jnp.bfloat16), yT_ref[sl], preferred_element_type=jnp.float32)
             return acc, num
 
-        acc, num = lax.fori_loop(
-            0,
-            nq,
-            second,
-            (jnp.zeros((bs, bs), jnp.float32), jnp.zeros((bs, yT_ref.shape[2]), jnp.float32)),
+        acc, num = _pair_loop(
+            cnt, second, (jnp.zeros((bs, bs), jnp.float32), jnp.zeros((bs, yT_ref.shape[2]), jnp.float32))
         )
         tot = jnp.sum(acc, axis=1, keepdims=True)
         xf = xs.astype(jnp.float32)
@@ -144,8 +145,7 @@
     nslot = peers * cap
     most = pair_slots.shape[1]
     log_mass = -math.log(peers * nblk * bs)
-    chunks = most // CHUNK
-    assert most % CHUNK == 0
+    assert most % TAIL == 0
 
     wanted = fetch_blocks[0]
     me = lax.axis_index("blocks")
@@ -190,7 +190,7 @@
     flat_slots = pair_slots.reshape(-1)
 
     vmem = 48 * 1024 * 1024
-    scratch = [pltpu.VMEM((nslot, 1, bs), jnp.float32), pltpu.VMEM((chunks, bs, CHUNK * bs), jnp.float32)]
+    scratch = [pltpu.VMEM((nslot, 1, bs), jnp.float32), pltpu.VMEM((most, bs, bs), jnp.float32)]
     gather_all = peers * nslot * bs * 4 <= (1 << 20)
     copies = peers if gather_all else 1
     sweep = pl.pallas_call(

time: 105 us -> 108 us (1.029)
  the two profiles are of different devices: /device:TPU:0 before, /device:TPU:26 now
where the time goes in v3:
time: 108 us; the launch traced here: 109 us
  Pallas kernels  52.8 us (49%)
  starting transfers between devices  23.1 us (21%)
  waiting for transfers between devices  22 us (20%)
  local copies, waits for them, and re-layouts  6.87 us (6%)
  other arithmetic  3.33 us (3%)
    pallas_call x2, Pallas kernels, local(): sweep(flat_slots, pair_counts, source_rows, slot_coords, slot_potential -...  33.7 us
    pallas_call x1, Pallas kernels, local(): final(flat_slots, pair_counts, source_rows, source_coords, slot_coords, s...  19.1 us
    all_to_all x2, waiting for transfers between devices, local(): lax.all_to_all(lse, 'blocks', split_axis=0, concat_axis=0, tiled=True)  13.2 us
    all_to_all x2, starting transfers between devices, local(): lax.all_to_all(lse, 'blocks', split_axis=0, concat_axis=0, tiled=True)  10.2 us
    all_to_all x1, starting transfers between devices, local(): lax.all_to_all(send, 'blocks', split_axis=0, concat_axis=0, tiled=True)  6.83 us
    all_to_all x1, waiting for transfers between devices, local(): lax.all_to_all(send, 'blocks', split_axis=0, concat_axis=0, tiled=True)  6.37 us
    all_to_all x1, starting transfers between devices, local(): lax.all_to_all(jnp.broadcast_to(wanted[None], (peers, peers, cap)), 'bloc...  6.07 us
    unnamed x15, local copies, waits for them, and re-layouts  2.96 us
  transfers between devices with their start and end apart: 4, of which 4 were waited for; matrix products, arithmetic and copies ran while one was open for 2% of the time, Pallas kernels for 0%

profile of v3, /device:TPU:26, one launch (start us, length us, event | category | flops | bytes accessed | tf_op | source)
XLA Modules:
  0.0 109.1 jit_solution(8094053688930725229)
XLA Ops:
  0.6 0.0 copy-start.4
  0.6 0.0 copy-start.2
  0.7 0.7 copy-done.4
  1.3 0.6 broadcast_in_dim.133
  1.9 6.1 %all-to-all-start = ((s32[16,16,2]{1,2,0:T(2,128)}), s32[16,16,2]{1,2,0:T(2,128)S(1)}, u32[]{:S(2)}, u32[]{:S(2)}) async-start(s32[16,16,2]{1,2,0:T(2,128)} %broadcast_in_dim.133), calls=%async_computation | async-start | bytes 32768 | tf_op jit(solution)/shard_map/all_to_all | solution.py:152
  8.0 0.7 reduce-precision_convert_fusion.1
  8.7 0.0 copy-done.2
  8.8 2.5 %all-to-all-done = s32[16,16,2]{1,2,0:T(2,128)S(1)} async-done(((s32[16,16,2]{1,2,0:T(2,128)}), s32[16,16,2]{1,2,0:T(2,128)S(1)}, u32[]{:S(2)}, u32[]{:S(2)}) %all-to-all-start) | async-done | bytes 2080 | tf_op jit(solution)/shard_map/all_to_all | solution.py:152
  11.3 0.4 fusion.19
  11.7 0.1 squeeze.9
  11.8 0.6 gather_fusion
  12.5 0.9 copy.88
  13.4 0.0 copy-start
  13.4 6.8 %all-to-all-start.1 = ((bf16[16,2,33,128]{3,1,2,0:T(2,128)(2,1)}), bf16[16,2,33,128]{3,1,2,0:T(2,128)(2,1)S(1)}, u32[]{:S(2)}, u32[]{:S(2)}) async-start(bf16[16,2,33,128]{3,1,2,0:T(2,128)(2,1)} %copy.88), calls=%async_computation.1 | async-start | bytes 540672 | tf_op jit(solution)/shard_map/all_to_all | solution.py:170
  20.2 0.0 copy-start.5
  20.2 0.1 pad.4.clone
  20.3 0.1 pad.3.clone
  20.4 0.5 copy-done.5
  20.9 0.1 reshape.291.slots_ref
  21.0 0.0 copy-done
  21.0 0.2 copy.100
  21.2 0.1 concatenate.12.clone
  21.2 6.4 %all-to-all-done.1 = bf16[16,2,33,128]{3,1,2,0:T(2,128)(2,1)S(1)} async-done(((bf16[16,2,33,128]{3,1,2,0:T(2,128)(2,1)}), bf16[16,2,33,128]{3,1,2,0:T(2,128)(2,1)S(1)}, u32[]{:S(2)}, u32[]{:S(2)}) %all-to-all-start.1) | async-done | bytes 270368 | tf_op jit(solution)/shard_map/all_to_all | solution.py:170
  27.7 0.1 multiply_reduce_fusion
  27.9 0.1 maximum_maximum_fusion.y_ref
  28.0 0.0 copy-start.1
  28.0 0.6 copy-done.1
  28.7 16.9 %shard_map.85 = f32[16,32,1,128]{3,2,1,0:T(1,128)} custom-call(s32[256]{0:T(256)S(1)} %reshape.291.slots_ref, s32[8]{0:T(128)S(1)} %copy-done.1, bf16[8,128,32]{2,1,0:T(8,128)(2,1)S(1)} %bitcast.70, bf16[32,32,128]{2,1,0:T(8,128)(2,1)S(1)} %maximum_maximum_fusion.y_ref, f32[32,1,128]{2,1,0:T(1,128)S(1)} %get-tuple-element.11.h_ref, ...), custom_call_target="tpu_custom_call" | custom-call | tf_op jit(solution)/shard_map/pallas_call | solution.py:227
  45.5 5.1 %all-to-all-start.2 = ((f32[16,32,1,128]{3,2,1,0:T(1,128)}), f32[16,32,1,128]{3,2,1,0:T(1,128)S(1)}, u32[]{:S(2)}, u32[]{:S(2)}) async-start(f32[16,32,1,128]{3,2,1,0:T(1,128)} %shard_map.85), calls=%async_computation.2 | async-start | bytes 524288 | tf_op jit(solution)/shard_map/all_to_all | solution.py:231
  50.6 0.1 copy.91
  50.7 0.1 copy.90
  50.8 0.1 copy.95
  50.9 0.1 broadcast_compare_fusion
  51.0 6.9 %all-to-all-done.2 = f32[16,32,1,128]{3,2,1,0:T(1,128)S(1)} async-done(((f32[16,32,1,128]{3,2,1,0:T(1,128)}), f32[16,32,1,128]{3,2,1,0:T(1,128)S(1)}, u32[]{:S(2)}, u32[]{:S(2)}) %all-to-all-start.2) | async-done | bytes 262176 | tf_op jit(solution)/shard_map/all_to_all | solution.py:231
  57.9 0.2 copy.92
  58.1 0.2 select_reduce_fusion.3
  58.3 0.3 select_reduce_fusion.2
  58.6 0.1 fusion.17
  58.6 16.9 %shard_map.86 = f32[16,32,1,128]{3,2,1,0:T(1,128)} custom-call(s32[256]{0:T(256)S(1)} %reshape.291.slots_ref, s32[8]{0:T(128)S(1)} %copy-done.1, bf16[8,128,32]{2,1,0:T(8,128)(2,1)S(1)} %bitcast.71, bf16[32,32,128]{2,1,0:T(8,128)(2,1)S(1)} %maximum_maximum_fusion.y_ref, f32[32,1,128]{2,1,0:T(1,128)S(1)} %get-tuple-element.9.h_ref, ...), custom_call_target="tpu_custom_call" | custom-call | tf_op jit(solution)/shard_map/pallas_call | solution.py:227
  75.5 5.1 %all-to-all-start.3 = ((f32[16,32,1,128]{3,2,1,0:T(1,128)}), f32[16,32,1,128]{3,2,1,0:T(1,128)S(1)}, u32[]{:S(2)}, u32[]{:S(2)}) async-start(f32[16,32,1,128]{3,2,1,0:T(1,128)} %shard_map.86), calls=%async_computation.3 | async-start | bytes 524288 | tf_op jit(solution)/shard_map/all_to_all | solution.py:231
  80.6 0.1 fusion.20
  80.7 0.5 copy.101
  81.2 0.3 concatenate.15.clone.yT_ref
  81.6 6.3 %all-to-all-done.3 = f32[16,32,1,128]{3,2,1,0:T(1,128)S(1)} async-done(((f32[16,32,1,128]{3,2,1,0:T(1,128)}), f32[16,32,1,128]{3,2,1,0:T(1,128)S(1)}, u32[]{:S(2)}, u32[]{:S(2)}) %all-to-all-start.3) | async-done | bytes 262176 | tf_op jit(solution)/shard_map/all_to_all | solution.py:231
  87.9 0.1 select_reduce_fusion.7
  88.0 0.1 select_reduce_fusion.6
  88.1 0.1 select_reduce_fusion.4
  88.2 0.2 copy.93
  88.4 0.2 select_reduce_fusion.1
  88.6 0.0 copy-start.3
  88.7 0.3 select_reduce_fusion
  88.9 0.4 copy-done.3
  89.3 0.6 fusion.10
  89.9 0.1 fusion.4.h_ref
  90.0 19.1 %shard_map.87 = (f32[8,1,128]{2,1,0:T(1,128)}, f32[30,1024]{1,0:T(8,128)}) custom-call(s32[256]{0:T(256)S(1)} %reshape.291.slots_ref, s32[8]{0:T(128)S(1)} %copy-done.1, bf16[8,128,32]{2,1,0:T(8,128)(2,1)S(1)} %bitcast.72, bf16[30,1024]{1,0:T(8,128)(2,1)S(1)} %copy-done, bf16[32,32,128]{2,1,0:T(8,128)(2,1)S(1)} %maximum_maximum_fusion.y_ref, ...), custom_call_target="tpu_custom_call" | custom-call | tf_op jit(solution)/shard_map/pallas_call | solution.py:248
  (20 shorter events, 0.3 us)
Async XLA Ops:
  0.6 0.7 copy-start.4
  0.6 8.1 %copy-start.2 = (bf16[30,1024]{1,0:T(8,128)(2,1)S(1)}, bf16[30,1024]{1,0:T(8,128)(2,1)}, u32[]{:S(2)}) copy-start(bf16[30,1024]{1,0:T(8,128)(2,1)} %param.7) | copy-start | bytes 184324
  1.9 9.4 %all-to-all-start = ((s32[16,16,2]{1,2,0:T(2,128)}), s32[16,16,2]{1,2,0:T(2,128)S(1)}, u32[]{:S(2)}, u32[]{:S(2)}) async-start(s32[16,16,2]{1,2,0:T(2,128)} %broadcast_in_dim.133), calls=%async_computation | async-start | bytes 32768 | tf_op jit(solution)/shard_map/all_to_all | solution.py:152
  13.4 7.6 %copy-start = (bf16[30,1024]{1,0:T(8,128)(2,1)S(1)}, bf16[30,1024]{1,0:T(8,128)(2,1)}, u32[]{:S(2)}) copy-start(bf16[30,1024]{1,0:T(8,128)(2,1)} %x_ref.1) | copy-start | bytes 184324
  13.4 14.2 %all-to-all-start.1 = ((bf16[16,2,33,128]{3,1,2,0:T(2,128)(2,1)}), bf16[16,2,33,128]{3,1,2,0:T(2,128)(2,1)S(1)}, u32[]{:S(2)}, u32[]{:S(2)}) async-start(bf16[16,2,33,128]{3,1,2,0:T(2,128)(2,1)} %copy.88), calls=%async_computation.1 | async-start | bytes 540672 | tf_op jit(solution)/shard_map/all_to_all | solution.py:170
  20.2 0.7 copy-start.5
  28.0 0.7 copy-start.1
  45.5 12.4 %all-to-all-start.2 = ((f32[16,32,1,128]{3,2,1,0:T(1,128)}), f32[16,32,1,128]{3,2,1,0:T(1,128)S(1)}, u32[]{:S(2)}, u32[]{:S(2)}) async-start(f32[16,32,1,128]{3,2,1,0:T(1,128)} %shard_map.85), calls=%async_computation.2 | async-start | bytes 524288 | tf_op jit(solution)/shard_map/all_to_all | solution.py:231
  75.5 12.4 %all-to-all-start.3 = ((f32[16,32,1,128]{3,2,1,0:T(1,128)}), f32[16,32,1,128]{3,2,1,0:T(1,128)S(1)}, u32[]{:S(2)}, u32[]{:S(2)}) async-start(f32[16,32,1,128]{3,2,1,0:T(1,128)} %shard_map.86), calls=%async_computation.3 | async-start | bytes 524288 | tf_op jit(solution)/shard_map/all_to_all | solution.py:231
  88.6 0.7 copy-start.3

commit v4 on v3

--- a/solution.py
+++ b/solution.py
@@ -12,8 +12,8 @@
 
 floor_value = -1e30
 PADDED = 32
-CHUNK = 8
-TAIL = 2
+CHUNK = 16
+TAIL = 8
 LOG2E = 1.4426950408889634
 LN2 = 0.6931471805599453
 

time: 108 us -> 98.2 us (0.909)
  the two profiles are of different devices: /device:TPU:26 before, /device:TPU:2 now
where the time goes in v4:
time: 98.2 us; the launch traced here: 97.3 us
  Pallas kernels  36.1 us (37%)
  waiting for transfers between devices  33.3 us (34%)
  starting transfers between devices  16.7 us (17%)
  local copies, waits for them, and re-layouts  6.88 us (7%)
  other arithmetic  3.34 us (3%)
    pallas_call x2, Pallas kernels, local(): sweep(flat_slots, pair_counts, source_rows, slot_coords, slot_potential -...  23.9 us
    all_to_all x2, waiting for transfers between devices, local(): lax.all_to_all(lse, 'blocks', split_axis=0, concat_axis=0, tiled=True)  18.6 us
    pallas_call x1, Pallas kernels, local(): final(flat_slots, pair_counts, source_rows, source_coords, slot_coords, s...  12.2 us
    all_to_all x1, waiting for transfers between devices, local(): lax.all_to_all(send, 'blocks', split_axis=0, concat_axis=0, tiled=True)  9.07 us
    all_to_all x2, starting transfers between devices, local(): lax.all_to_all(lse, 'blocks', split_axis=0, concat_axis=0, tiled=True)  7.06 us
    all_to_all x1, starting transfers between devices, local(): lax.all_to_all(jnp.broadcast_to(wanted[None], (peers, peers, cap)), 'bloc...  5.94 us
    all_to_all x1, waiting for transfers between devices, local(): lax.all_to_all(jnp.broadcast_to(wanted[None], (peers, peers, cap)), 'bloc...  5.66 us
    all_to_all x1, starting transfers between devices, local(): lax.all_to_all(send, 'blocks', split_axis=0, concat_axis=0, tiled=True)  3.66 us
  transfers between devices with their start and end apart: 4, of which 4 were waited for; matrix products, arithmetic and copies ran while one was open for 3% of the time, Pallas kernels for 0%

profile of v4, /device:TPU:2, one launch (start us, length us, event | category | flops | bytes accessed | tf_op | source)
XLA Modules:
  0.0 97.3 jit_solution(17160965640838461832)
XLA Ops:
  0.6 0.0 copy-start.4
  0.6 0.0 copy-start.2
  0.7 0.7 copy-done.4
  1.3 0.6 broadcast_in_dim.133
  1.9 5.9 %all-to-all-start = ((s32[16,16,2]{1,2,0:T(2,128)}), s32[16,16,2]{1,2,0:T(2,128)S(1)}, u32[]{:S(2)}, u32[]{:S(2)}) async-start(s32[16,16,2]{1,2,0:T(2,128)} %broadcast_in_dim.133), calls=%async_computation | async-start | bytes 32768 | tf_op jit(solution)/shard_map/all_to_all | solution.py:152
  7.9 0.7 reduce-precision_convert_fusion.1
  8.6 0.0 copy-done.2
  8.7 5.7 %all-to-all-done = s32[16,16,2]{1,2,0:T(2,128)S(1)} async-done(((s32[16,16,2]{1,2,0:T(2,128)}), s32[16,16,2]{1,2,0:T(2,128)S(1)}, u32[]{:S(2)}, u32[]{:S(2)}) %all-to-all-start) | async-done | bytes 2080 | tf_op jit(solution)/shard_map/all_to_all | solution.py:152
  14.4 0.4 fusion.19
  14.8 0.1 squeeze.9
  14.9 0.6 gather_fusion
  15.5 0.9 copy.88
  16.5 0.0 copy-start
  16.5 3.7 %all-to-all-start.1 = ((bf16[16,2,33,128]{3,1,2,0:T(2,128)(2,1)}), bf16[16,2,33,128]{3,1,2,0:T(2,128)(2,1)S(1)}, u32[]{:S(2)}, u32[]{:S(2)}) async-start(bf16[16,2,33,128]{3,1,2,0:T(2,128)(2,1)} %copy.88), calls=%async_computation.1 | async-start | bytes 540672 | tf_op jit(solution)/shard_map/all_to_all | solution.py:170
  20.1 0.0 copy-start.5
  20.1 0.1 pad.4.clone
  20.2 0.1 pad.3.clone
  20.3 0.5 copy-done.5
  20.8 0.1 reshape.291.slots_ref
  20.9 0.0 copy-done
  20.9 0.2 copy.100
  21.1 0.1 concatenate.12.clone
  21.2 9.1 %all-to-all-done.1 = bf16[16,2,33,128]{3,1,2,0:T(2,128)(2,1)S(1)} async-done(((bf16[16,2,33,128]{3,1,2,0:T(2,128)(2,1)}), bf16[16,2,33,128]{3,1,2,0:T(2,128)(2,1)S(1)}, u32[]{:S(2)}, u32[]{:S(2)}) %all-to-all-start.1) | async-done | bytes 270368 | tf_op jit(solution)/shard_map/all_to_all | solution.py:170
  30.3 0.1 multiply_reduce_fusion
  30.5 0.1 maximum_maximum_fusion.y_ref
  30.6 0.0 copy-start.1
  30.6 0.6 copy-done.1
  31.3 12.0 %shard_map.85 = f32[16,32,1,128]{3,2,1,0:T(1,128)} custom-call(s32[256]{0:T(256)S(1)} %reshape.291.slots_ref, s32[8]{0:T(128)S(1)} %copy-done.1, bf16[8,128,32]{2,1,0:T(8,128)(2,1)S(1)} %bitcast.70, bf16[32,32,128]{2,1,0:T(8,128)(2,1)S(1)} %maximum_maximum_fusion.y_ref, f32[32,1,128]{2,1,0:T(1,128)S(1)} %get-tuple-element.11.h_ref, ...), custom_call_target="tpu_custom_call" | custom-call | tf_op jit(solution)/shard_map/pallas_call | solution.py:227
  43.3 3.5 %all-to-all-start.2 = ((f32[16,32,1,128]{3,2,1,0:T(1,128)}), f32[16,32,1,128]{3,2,1,0:T(1,128)S(1)}, u32[]{:S(2)}, u32[]{:S(2)}) async-start(f32[16,32,1,128]{3,2,1,0:T(1,128)} %shard_map.85), calls=%async_computation.2 | async-start | bytes 524288 | tf_op jit(solution)/shard_map/all_to_all | solution.py:231
  46.8 0.1 copy.91
  46.9 0.1 copy.90
  47.0 0.1 copy.95
  47.1 0.1 broadcast_compare_fusion
  47.2 9.6 %all-to-all-done.2 = f32[16,32,1,128]{3,2,1,0:T(1,128)S(1)} async-done(((f32[16,32,1,128]{3,2,1,0:T(1,128)}), f32[16,32,1,128]{3,2,1,0:T(1,128)S(1)}, u32[]{:S(2)}, u32[]{:S(2)}) %all-to-all-start.2) | async-done | bytes 262176 | tf_op jit(solution)/shard_map/all_to_all | solution.py:231
  56.8 0.2 copy.92
  56.9 0.2 select_reduce_fusion.3
  57.2 0.3 select_reduce_fusion.2
  57.4 0.1 fusion.17
  57.5 12.0 %shard_map.86 = f32[16,32,1,128]{3,2,1,0:T(1,128)} custom-call(s32[256]{0:T(256)S(1)} %reshape.291.slots_ref, s32[8]{0:T(128)S(1)} %copy-done.1, bf16[8,128,32]{2,1,0:T(8,128)(2,1)S(1)} %bitcast.71, bf16[32,32,128]{2,1,0:T(8,128)(2,1)S(1)} %maximum_maximum_fusion.y_ref, f32[32,1,128]{2,1,0:T(1,128)S(1)} %get-tuple-element.9.h_ref, ...), custom_call_target="tpu_custom_call" | custom-call | tf_op jit(solution)/shard_map/pallas_call | solution.py:227
  69.5 3.5 %all-to-all-start.3 = ((f32[16,32,1,128]{3,2,1,0:T(1,128)}), f32[16,32,1,128]{3,2,1,0:T(1,128)S(1)}, u32[]{:S(2)}, u32[]{:S(2)}) async-start(f32[16,32,1,128]{3,2,1,0:T(1,128)} %shard_map.86), calls=%async_computation.3 | async-start | bytes 524288 | tf_op jit(solution)/shard_map/all_to_all | solution.py:231
  73.0 0.1 fusion.20
  73.1 0.5 copy.101
  73.6 0.3 concatenate.15.clone.yT_ref
  73.9 9.0 %all-to-all-done.3 = f32[16,32,1,128]{3,2,1,0:T(1,128)S(1)} async-done(((f32[16,32,1,128]{3,2,1,0:T(1,128)}), f32[16,32,1,128]{3,2,1,0:T(1,128)S(1)}, u32[]{:S(2)}, u32[]{:S(2)}) %all-to-all-start.3) | async-done | bytes 262176 | tf_op jit(solution)/shard_map/all_to_all | solution.py:231
  83.0 0.1 select_reduce_fusion.7
  83.1 0.1 select_reduce_fusion.6
  83.2 0.1 select_reduce_fusion.4
  83.3 0.2 copy.93
  83.5 0.2 select_reduce_fusion.1
  83.7 0.0 copy-start.3
  83.8 0.3 select_reduce_fusion
  84.0 0.4 copy-done.3
  84.4 0.6 fusion.10
  85.0 0.1 fusion.4.h_ref
  85.1 12.2 %shard_map.87 = (f32[8,1,128]{2,1,0:T(1,128)}, f32[30,1024]{1,0:T(8,128)}) custom-call(s32[256]{0:T(256)S(1)} %reshape.291.slots_ref, s32[8]{0:T(128)S(1)} %copy-done.1, bf16[8,128,32]{2,1,0:T(8,128)(2,1)S(1)} %bitcast.72, bf16[30,1024]{1,0:T(8,128)(2,1)S(1)} %copy-done, bf16[32,32,128]{2,1,0:T(8,128)(2,1)S(1)} %maximum_maximum_fusion.y_ref, ...), custom_call_target="tpu_custom_call" | custom-call | tf_op jit(solution)/shard_map/pallas_call | solution.py:248
  (20 shorter events, 0.3 us)
Async XLA Ops:
  0.6 0.7 copy-start.4
  0.6 8.0 %copy-start.2 = (bf16[30,1024]{1,0:T(8,128)(2,1)S(1)}, bf16[30,1024]{1,0:T(8,128)(2,1)}, u32[]{:S(2)}) copy-start(bf16[30,1024]{1,0:T(8,128)(2,1)} %param.7) | copy-start | bytes 184324
  1.9 12.4 %all-to-all-start = ((s32[16,16,2]{1,2,0:T(2,128)}), s32[16,16,2]{1,2,0:T(2,128)S(1)}, u32[]{:S(2)}, u32[]{:S(2)}) async-start(s32[16,16,2]{1,2,0:T(2,128)} %broadcast_in_dim.133), calls=%async_computation | async-start | bytes 32768 | tf_op jit(solution)/shard_map/all_to_all | solution.py:152
  16.5 4.4 %copy-start = (bf16[30,1024]{1,0:T(8,128)(2,1)S(1)}, bf16[30,1024]{1,0:T(8,128)(2,1)}, u32[]{:S(2)}) copy-start(bf16[30,1024]{1,0:T(8,128)(2,1)} %x_ref.1) | copy-start | bytes 184324
  16.5 13.8 %all-to-all-start.1 = ((bf16[16,2,33,128]{3,1,2,0:T(2,128)(2,1)}), bf16[16,2,33,128]{3,1,2,0:T(2,128)(2,1)S(1)}, u32[]{:S(2)}, u32[]{:S(2)}) async-start(bf16[16,2,33,128]{3,1,2,0:T(2,128)(2,1)} %copy.88), calls=%async_computation.1 | async-start | bytes 540672 | tf_op jit(solution)/shard_map/all_to_all | solution.py:170
  20.1 0.7 copy-start.5
  30.6 0.7 copy-start.1
  43.3 13.5 %all-to-all-start.2 = ((f32[16,32,1,128]{3,2,1,0:T(1,128)}), f32[16,32,1,128]{3,2,1,0:T(1,128)S(1)}, u32[]{:S(2)}, u32[]{:S(2)}) async-start(f32[16,32,1,128]{3,2,1,0:T(1,128)} %shard_map.85), calls=%async_computation.2 | async-start | bytes 524288 | tf_op jit(solution)/shard_map/all_to_all | solution.py:231
  69.5 13.5 %all-to-all-start.3 = ((f32[16,32,1,128]{3,2,1,0:T(1,128)}), f32[16,32,1,128]{3,2,1,0:T(1,128)S(1)}, u32[]{:S(2)}, u32[]{:S(2)}) async-start(f32[16,32,1,128]{3,2,1,0:T(1,128)} %shard_map.86), calls=%async_computation.3 | async-start | bytes 524288 | tf_op jit(solution)/shard_map/all_to_all | solution.py:231
  83.7 0.7 copy-start.3

commit v5 on v4

--- a/solution.py
+++ b/solution.py
@@ -12,8 +12,8 @@
 
 floor_value = -1e30
 PADDED = 32
-CHUNK = 16
-TAIL = 8
+CHUNK = 32
+TAIL = 16
 LOG2E = 1.4426950408889634
 LN2 = 0.6931471805599453
 

time: 98.2 us -> 96.7 us (0.985)
  the two profiles are of different devices: /device:TPU:2 before, /device:TPU:0 now
where the time goes in v5:
time: 96.7 us; the launch traced here: 95.9 us
  waiting for transfers between devices  33.4 us (35%)
  Pallas kernels  29.2 us (30%)
  starting transfers between devices  22.1 us (23%)
  local copies, waits for them, and re-layouts  6.88 us (7%)
  other arithmetic  3.34 us (3%)
    pallas_call x2, Pallas kernels, local(): sweep(flat_slots, pair_counts, source_rows, slot_coords, slot_potential -...  19.8 us
    all_to_all x2, waiting for transfers between devices, local(): lax.all_to_all(lse, 'blocks', split_axis=0, concat_axis=0, tiled=True)  18.7 us
    all_to_all x2, starting transfers between devices, local(): lax.all_to_all(lse, 'blocks', split_axis=0, concat_axis=0, tiled=True)  11 us
    pallas_call x1, Pallas kernels, local(): final(flat_slots, pair_counts, source_rows, source_coords, slot_coords, s...  9.41 us
    all_to_all x1, waiting for transfers between devices, local(): lax.all_to_all(send, 'blocks', split_axis=0, concat_axis=0, tiled=True)  9.07 us
    all_to_all x1, starting transfers between devices, local(): lax.all_to_all(jnp.broadcast_to(wanted[None], (peers, peers, cap)), 'bloc...  7.41 us
    all_to_all x1, waiting for transfers between devices, local(): lax.all_to_all(jnp.broadcast_to(wanted[None], (peers, peers, cap)), 'bloc...  5.66 us
    all_to_all x1, starting transfers between devices, local(): lax.all_to_all(send, 'blocks', split_axis=0, concat_axis=0, tiled=True)  3.66 us
  transfers between devices with their start and end apart: 4, of which 4 were waited for; matrix products, arithmetic and copies ran while one was open for 3% of the time, Pallas kernels for 0%

profile of v5, /device:TPU:0, one launch (start us, length us, event | category | flops | bytes accessed | tf_op | source)
XLA Modules:
  0.0 95.9 jit_solution(17090476167621715826)
XLA Ops:
  0.6 0.0 copy-start.4
  0.6 0.0 copy-start.2
  0.7 0.7 copy-done.4
  1.3 0.6 broadcast_in_dim.133
  1.9 7.4 %all-to-all-start = ((s32[16,16,2]{1,2,0:T(2,128)}), s32[16,16,2]{1,2,0:T(2,128)S(1)}, u32[]{:S(2)}, u32[]{:S(2)}) async-start(s32[16,16,2]{1,2,0:T(2,128)} %broadcast_in_dim.133), calls=%async_computation | async-start | bytes 32768 | tf_op jit(solution)/shard_map/all_to_all | solution.py:152
  9.3 0.7 reduce-precision_convert_fusion.1
  10.1 0.0 copy-done.2
  10.2 5.7 %all-to-all-done = s32[16,16,2]{1,2,0:T(2,128)S(1)} async-done(((s32[16,16,2]{1,2,0:T(2,128)}), s32[16,16,2]{1,2,0:T(2,128)S(1)}, u32[]{:S(2)}, u32[]{:S(2)}) %all-to-all-start) | async-done | bytes 2080 | tf_op jit(solution)/shard_map/all_to_all | solution.py:152
  15.8 0.4 fusion.19
  16.3 0.1 squeeze.9
  16.4 0.6 gather_fusion
  17.0 0.9 copy.88
  17.9 0.0 copy-start
  17.9 3.7 %all-to-all-start.1 = ((bf16[16,2,33,128]{3,1,2,0:T(2,128)(2,1)}), bf16[16,2,33,128]{3,1,2,0:T(2,128)(2,1)S(1)}, u32[]{:S(2)}, u32[]{:S(2)}) async-start(bf16[16,2,33,128]{3,1,2,0:T(2,128)(2,1)} %copy.88), calls=%async_computation.1 | async-start | bytes 540672 | tf_op jit(solution)/shard_map/all_to_all | solution.py:170
  21.6 0.0 copy-start.5
  21.6 0.1 pad.4.clone
  21.7 0.1 pad.3.clone
  21.8 0.5 copy-done.5
  22.3 0.1 reshape.291.slots_ref
  22.4 0.0 copy-done
  22.4 0.2 copy.100
  22.6 0.1 concatenate.12.clone
  22.6 9.1 %all-to-all-done.1 = bf16[16,2,33,128]{3,1,2,0:T(2,128)(2,1)S(1)} async-done(((bf16[16,2,33,128]{3,1,2,0:T(2,128)(2,1)}), bf16[16,2,33,128]{3,1,2,0:T(2,128)(2,1)S(1)}, u32[]{:S(2)}, u32[]{:S(2)}) %all-to-all-start.1) | async-done | bytes 270368 | tf_op jit(solution)/shard_map/all_to_all | solution.py:170
  31.8 0.1 multiply_reduce_fusion
  32.0 0.1 maximum_maximum_fusion.y_ref
  32.1 0.0 copy-start.1
  32.1 0.6 copy-done.1
  32.8 9.9 %shard_map.85 = f32[16,32,1,128]{3,2,1,0:T(1,128)} custom-call(s32[256]{0:T(256)S(1)} %reshape.291.slots_ref, s32[8]{0:T(128)S(1)} %copy-done.1, bf16[8,128,32]{2,1,0:T(8,128)(2,1)S(1)} %bitcast.70, bf16[32,32,128]{2,1,0:T(8,128)(2,1)S(1)} %maximum_maximum_fusion.y_ref, f32[32,1,128]{2,1,0:T(1,128)S(1)} %get-tuple-element.11.h_ref, ...), custom_call_target="tpu_custom_call" | custom-call | tf_op jit(solution)/shard_map/pallas_call | solution.py:227
  42.7 5.5 %all-to-all-start.2 = ((f32[16,32,1,128]{3,2,1,0:T(1,128)}), f32[16,32,1,128]{3,2,1,0:T(1,128)S(1)}, u32[]{:S(2)}, u32[]{:S(2)}) async-start(f32[16,32,1,128]{3,2,1,0:T(1,128)} %shard_map.85), calls=%async_computation.2 | async-start | bytes 524288 | tf_op jit(solution)/shard_map/all_to_all | solution.py:231
  48.2 0.1 copy.91
  48.3 0.1 copy.90
  48.4 0.1 copy.95
  48.5 0.1 broadcast_compare_fusion
  48.6 9.6 %all-to-all-done.2 = f32[16,32,1,128]{3,2,1,0:T(1,128)S(1)} async-done(((f32[16,32,1,128]{3,2,1,0:T(1,128)}), f32[16,32,1,128]{3,2,1,0:T(1,128)S(1)}, u32[]{:S(2)}, u32[]{:S(2)}) %all-to-all-start.2) | async-done | bytes 262176 | tf_op jit(solution)/shard_map/all_to_all | solution.py:231
  58.2 0.2 copy.92
  58.4 0.2 select_reduce_fusion.3
  58.6 0.3 select_reduce_fusion.2
  58.9 0.1 fusion.17
  58.9 9.9 %shard_map.86 = f32[16,32,1,128]{3,2,1,0:T(1,128)} custom-call(s32[256]{0:T(256)S(1)} %reshape.291.slots_ref, s32[8]{0:T(128)S(1)} %copy-done.1, bf16[8,128,32]{2,1,0:T(8,128)(2,1)S(1)} %bitcast.71, bf16[32,32,128]{2,1,0:T(8,128)(2,1)S(1)} %maximum_maximum_fusion.y_ref, f32[32,1,128]{2,1,0:T(1,128)S(1)} %get-tuple-element.9.h_ref, ...), custom_call_target="tpu_custom_call" | custom-call | tf_op jit(solution)/shard_map/pallas_call | solution.py:227
  68.9 5.5 %all-to-all-start.3 = ((f32[16,32,1,128]{3,2,1,0:T(1,128)}), f32[16,32,1,128]{3,2,1,0:T(1,128)S(1)}, u32[]{:S(2)}, u32[]{:S(2)}) async-start(f32[16,32,1,128]{3,2,1,0:T(1,128)} %shard_map.86), calls=%async_computation.3 | async-start | bytes 524288 | tf_op jit(solution)/shard_map/all_to_all | solution.py:231
  74.4 0.1 fusion.20
  74.5 0.5 copy.101
  75.0 0.3 concatenate.15.clone.yT_ref
  75.3 9.1 %all-to-all-done.3 = f32[16,32,1,128]{3,2,1,0:T(1,128)S(1)} async-done(((f32[16,32,1,128]{3,2,1,0:T(1,128)}), f32[16,32,1,128]{3,2,1,0:T(1,128)S(1)}, u32[]{:S(2)}, u32[]{:S(2)}) %all-to-all-start.3) | async-done | bytes 262176 | tf_op jit(solution)/shard_map/all_to_all | solution.py:231
  84.4 0.1 select_reduce_fusion.7
  84.5 0.1 select_reduce_fusion.6
  84.6 0.1 select_reduce_fusion.4
  84.8 0.2 copy.93
  84.9 0.2 select_reduce_fusion.1
  85.2 0.0 copy-start.3
  85.2 0.3 select_reduce_fusion
  85.4 0.4 copy-done.3
  85.8 0.6 fusion.10
  86.5 0.1 fusion.4.h_ref
  86.5 9.4 %shard_map.87 = (f32[8,1,128]{2,1,0:T(1,128)}, f32[30,1024]{1,0:T(8,128)}) custom-call(s32[256]{0:T(256)S(1)} %reshape.291.slots_ref, s32[8]{0:T(128)S(1)} %copy-done.1, bf16[8,128,32]{2,1,0:T(8,128)(2,1)S(1)} %bitcast.72, bf16[30,1024]{1,0:T(8,128)(2,1)S(1)} %copy-done, bf16[32,32,128]{2,1,0:T(8,128)(2,1)S(1)} %maximum_maximum_fusion.y_ref, ...), custom_call_target="tpu_custom_call" | custom-call | tf_op jit(solution)/shard_map/pallas_call | solution.py:248
  (20 shorter events, 0.3 us)
Async XLA Ops:
  0.6 0.7 copy-start.4
  0.6 9.4 %copy-start.2 = (bf16[30,1024]{1,0:T(8,128)(2,1)S(1)}, bf16[30,1024]{1,0:T(8,128)(2,1)}, u32[]{:S(2)}) copy-start(bf16[30,1024]{1,0:T(8,128)(2,1)} %param.7) | copy-start | bytes 184324
  1.9 13.9 %all-to-all-start = ((s32[16,16,2]{1,2,0:T(2,128)}), s32[16,16,2]{1,2,0:T(2,128)S(1)}, u32[]{:S(2)}, u32[]{:S(2)}) async-start(s32[16,16,2]{1,2,0:T(2,128)} %broadcast_in_dim.133), calls=%async_computation | async-start | bytes 32768 | tf_op jit(solution)/shard_map/all_to_all | solution.py:152
  17.9 4.4 %copy-start = (bf16[30,1024]{1,0:T(8,128)(2,1)S(1)}, bf16[30,1024]{1,0:T(8,128)(2,1)}, u32[]{:S(2)}) copy-start(bf16[30,1024]{1,0:T(8,128)(2,1)} %x_ref.1) | copy-start | bytes 184324
  17.9 13.8 %all-to-all-start.1 = ((bf16[16,2,33,128]{3,1,2,0:T(2,128)(2,1)}), bf16[16,2,33,128]{3,1,2,0:T(2,128)(2,1)S(1)}, u32[]{:S(2)}, u32[]{:S(2)}) async-start(bf16[16,2,33,128]{3,1,2,0:T(2,128)(2,1)} %copy.88), calls=%async_computation.1 | async-start | bytes 540672 | tf_op jit(solution)/shard_map/all_to_all | solution.py:170
  21.6 0.7 copy-start.5
  32.1 0.7 copy-start.1
  42.7 15.6 %all-to-all-start.2 = ((f32[16,32,1,128]{3,2,1,0:T(1,128)}), f32[16,32,1,128]{3,2,1,0:T(1,128)S(1)}, u32[]{:S(2)}, u32[]{:S(2)}) async-start(f32[16,32,1,128]{3,2,1,0:T(1,128)} %shard_map.85), calls=%async_computation.2 | async-start | bytes 524288 | tf_op jit(solution)/shard_map/all_to_all | solution.py:231
  68.9 15.5 %all-to-all-start.3 = ((f32[16,32,1,128]{3,2,1,0:T(1,128)}), f32[16,32,1,128]{3,2,1,0:T(1,128)S(1)}, u32[]{:S(2)}, u32[]{:S(2)}) async-start(f32[16,32,1,128]{3,2,1,0:T(1,128)} %shard_map.86), calls=%async_computation.3 | async-start | bytes 524288 | tf_op jit(solution)/shard_map/all_to_all | solution.py:231
  85.2 0.7 copy-start.3

commit v6 on v5

--- a/solution.py
+++ b/solution.py
@@ -13,7 +13,7 @@
 floor_value = -1e30
 PADDED = 32
 CHUNK = 32
-TAIL = 16
+TAIL = 32
 LOG2E = 1.4426950408889634
 LN2 = 0.6931471805599453
 

time: 96.7 us -> 99.3 us (1.027)
  Pallas kernels: 29.2 us -> 36 us
  starting transfers between devices: 22.1 us -> 18.1 us
    pallas_call x2, Pallas kernels: 19.8 us -> 25.4 us  [local(): sweep(flat_slots, pair_counts, source_rows, slot_coords, slot_potential -...]
    all_to_all x2, starting transfers between devices: 11 us -> 7.06 us  [local(): lax.all_to_all(lse, 'blocks', split_axis=0, concat_axis=0, tiled=True)]
    pallas_call x1, Pallas kernels: 9.41 us -> 10.6 us  [local(): final(flat_slots, pair_counts, source_rows, source_coords, slot_coords, s...]
where the time goes in v6:
time: 99.3 us; the launch traced here: 98.7 us
  Pallas kernels  36 us (36%)
  waiting for transfers between devices  33.3 us (34%)
  starting transfers between devices  18.1 us (18%)
  local copies, waits for them, and re-layouts  6.88 us (7%)
  other arithmetic  3.34 us (3%)
    pallas_call x2, Pallas kernels, local(): sweep(flat_slots, pair_counts, source_rows, slot_coords, slot_potential -...  25.4 us
    all_to_all x2, waiting for transfers between devices, local(): lax.all_to_all(lse, 'blocks', split_axis=0, concat_axis=0, tiled=True)  18.6 us
    pallas_call x1, Pallas kernels, local(): final(flat_slots, pair_counts, source_rows, source_coords, slot_coords, s...  10.6 us
    all_to_all x1, waiting for transfers between devices, local(): lax.all_to_all(send, 'blocks', split_axis=0, concat_axis=0, tiled=True)  9.07 us
    all_to_all x1, starting transfers between devices, local(): lax.all_to_all(jnp.broadcast_to(wanted[None], (peers, peers, cap)), 'bloc...  7.41 us
    all_to_all x2, starting transfers between devices, local(): lax.all_to_all(lse, 'blocks', split_axis=0, concat_axis=0, tiled=True)  7.06 us
    all_to_all x1, waiting for transfers between devices, local(): lax.all_to_all(jnp.broadcast_to(wanted[None], (peers, peers, cap)), 'bloc...  5.66 us
    all_to_all x1, starting transfers between devices, local(): lax.all_to_all(send, 'blocks', split_axis=0, concat_axis=0, tiled=True)  3.66 us
  transfers between devices with their start and end apart: 4, of which 4 were waited for; matrix products, arithmetic and copies ran while one was open for 3% of the time, Pallas kernels for 0%

profile of v6, /device:TPU:0, one launch (start us, length us, event | category | flops | bytes accessed | tf_op | source)
XLA Modules:
  0.0 98.7 jit_solution(2765792003272428048)
XLA Ops:
  0.6 0.0 copy-start.4
  0.6 0.0 copy-start.2
  0.7 0.7 copy-done.4
  1.3 0.6 broadcast_in_dim.133
  1.9 7.4 %all-to-all-start = ((s32[16,16,2]{1,2,0:T(2,128)}), s32[16,16,2]{1,2,0:T(2,128)S(1)}, u32[]{:S(2)}, u32[]{:S(2)}) async-start(s32[16,16,2]{1,2,0:T(2,128)} %broadcast_in_dim.133), calls=%async_computation | async-start | bytes 32768 | tf_op jit(solution)/shard_map/all_to_all | solution.py:152
  9.3 0.7 reduce-precision_convert_fusion.1
  10.1 0.0 copy-done.2
  10.2 5.7 %all-to-all-done = s32[16,16,2]{1,2,0:T(2,128)S(1)} async-done(((s32[16,16,2]{1,2,0:T(2,128)}), s32[16,16,2]{1,2,0:T(2,128)S(1)}, u32[]{:S(2)}, u32[]{:S(2)}) %all-to-all-start) | async-done | bytes 2080 | tf_op jit(solution)/shard_map/all_to_all | solution.py:152
  15.8 0.4 fusion.19
  16.3 0.1 squeeze.9
  16.4 0.6 gather_fusion
  17.0 0.9 copy.88
  17.9 0.0 copy-start
  17.9 3.7 %all-to-all-start.1 = ((bf16[16,2,33,128]{3,1,2,0:T(2,128)(2,1)}), bf16[16,2,33,128]{3,1,2,0:T(2,128)(2,1)S(1)}, u32[]{:S(2)}, u32[]{:S(2)}) async-start(bf16[16,2,33,128]{3,1,2,0:T(2,128)(2,1)} %copy.88), calls=%async_computation.1 | async-start | bytes 540672 | tf_op jit(solution)/shard_map/all_to_all | solution.py:170
  21.6 0.0 copy-start.5
  21.6 0.1 pad.4.clone
  21.7 0.1 pad.3.clone
  21.8 0.5 copy-done.5
  22.3 0.1 reshape.291.slots_ref
  22.4 0.0 copy-done
  22.4 0.2 copy.100
  22.6 0.1 concatenate.12.clone
  22.6 9.1 %all-to-all-done.1 = bf16[16,2,33,128]{3,1,2,0:T(2,128)(2,1)S(1)} async-done(((bf16[16,2,33,128]{3,1,2,0:T(2,128)(2,1)}), bf16[16,2,33,128]{3,1,2,0:T(2,128)(2,1)S(1)}, u32[]{:S(2)}, u32[]{:S(2)}) %all-to-all-start.1) | async-done | bytes 270368 | tf_op jit(solution)/shard_map/all_to_all | solution.py:170
  31.8 0.1 multiply_reduce_fusion
  32.0 0.1 maximum_maximum_fusion.y_ref
  32.1 0.0 copy-start.1
  32.1 0.6 copy-done.1
  32.8 12.7 %shard_map.85 = f32[16,32,1,128]{3,2,1,0:T(1,128)} custom-call(s32[256]{0:T(256)S(1)} %reshape.291.slots_ref, s32[8]{0:T(128)S(1)} %copy-done.1, bf16[8,128,32]{2,1,0:T(8,128)(2,1)S(1)} %bitcast.70, bf16[32,32,128]{2,1,0:T(8,128)(2,1)S(1)} %maximum_maximum_fusion.y_ref, f32[32,1,128]{2,1,0:T(1,128)S(1)} %get-tuple-element.11.h_ref, ...), custom_call_target="tpu_custom_call" | custom-call | tf_op jit(solution)/shard_map/pallas_call | solution.py:227
  45.5 3.5 %all-to-all-start.2 = ((f32[16,32,1,128]{3,2,1,0:T(1,128)}), f32[16,32,1,128]{3,2,1,0:T(1,128)S(1)}, u32[]{:S(2)}, u32[]{:S(2)}) async-start(f32[16,32,1,128]{3,2,1,0:T(1,128)} %shard_map.85), calls=%async_computation.2 | async-start | bytes 524288 | tf_op jit(solution)/shard_map/all_to_all | solution.py:231
  49.0 0.1 copy.91
  49.1 0.1 copy.90
  49.2 0.1 copy.95
  49.3 0.1 broadcast_compare_fusion
  49.4 9.6 %all-to-all-done.2 = f32[16,32,1,128]{3,2,1,0:T(1,128)S(1)} async-done(((f32[16,32,1,128]{3,2,1,0:T(1,128)}), f32[16,32,1,128]{3,2,1,0:T(1,128)S(1)}, u32[]{:S(2)}, u32[]{:S(2)}) %all-to-all-start.2) | async-done | bytes 262176 | tf_op jit(solution)/shard_map/all_to_all | solution.py:231
  59.0 0.2 copy.92
  59.2 0.2 select_reduce_fusion.3
  59.4 0.3 select_reduce_fusion.2
  59.6 0.1 fusion.17
  59.7 12.7 %shard_map.86 = f32[16,32,1,128]{3,2,1,0:T(1,128)} custom-call(s32[256]{0:T(256)S(1)} %reshape.291.slots_ref, s32[8]{0:T(128)S(1)} %copy-done.1, bf16[8,128,32]{2,1,0:T(8,128)(2,1)S(1)} %bitcast.71, bf16[32,32,128]{2,1,0:T(8,128)(2,1)S(1)} %maximum_maximum_fusion.y_ref, f32[32,1,128]{2,1,0:T(1,128)S(1)} %get-tuple-element.9.h_ref, ...), custom_call_target="tpu_custom_call" | custom-call | tf_op jit(solution)/shard_map/pallas_call | solution.py:227
  72.4 3.5 %all-to-all-start.3 = ((f32[16,32,1,128]{3,2,1,0:T(1,128)}), f32[16,32,1,128]{3,2,1,0:T(1,128)S(1)}, u32[]{:S(2)}, u32[]{:S(2)}) async-start(f32[16,32,1,128]{3,2,1,0:T(1,128)} %shard_map.86), calls=%async_computation.3 | async-start | bytes 524288 | tf_op jit(solution)/shard_map/all_to_all | solution.py:231
  76.0 0.1 fusion.20
  76.1 0.5 copy.101
  76.6 0.3 concatenate.15.clone.yT_ref
  76.9 9.0 %all-to-all-done.3 = f32[16,32,1,128]{3,2,1,0:T(1,128)S(1)} async-done(((f32[16,32,1,128]{3,2,1,0:T(1,128)}), f32[16,32,1,128]{3,2,1,0:T(1,128)S(1)}, u32[]{:S(2)}, u32[]{:S(2)}) %all-to-all-start.3) | async-done | bytes 262176 | tf_op jit(solution)/shard_map/all_to_all | solution.py:231
  86.0 0.1 select_reduce_fusion.7
  86.1 0.1 select_reduce_fusion.6
  86.2 0.1 select_reduce_fusion.4
  86.3 0.2 copy.93
  86.5 0.2 select_reduce_fusion.1
  86.7 0.0 copy-start.3
  86.7 0.3 select_reduce_fusion
  87.0 0.4 copy-done.3
  87.4 0.6 fusion.10
  88.0 0.1 fusion.4.h_ref
  88.1 10.6 %shard_map.87 = (f32[8,1,128]{2,1,0:T(1,128)}, f32[30,1024]{1,0:T(8,128)}) custom-call(s32[256]{0:T(256)S(1)} %reshape.291.slots_ref, s32[8]{0:T(128)S(1)} %copy-done.1, bf16[8,128,32]{2,1,0:T(8,128)(2,1)S(1)} %bitcast.72, bf16[30,1024]{1,0:T(8,128)(2,1)S(1)} %copy-done, bf16[32,32,128]{2,1,0:T(8,128)(2,1)S(1)} %maximum_maximum_fusion.y_ref, ...), custom_call_target="tpu_custom_call" | custom-call | tf_op jit(solution)/shard_map/pallas_call | solution.py:248
  (20 shorter events, 0.3 us)
Async XLA Ops:
  0.6 0.7 copy-start.4
  0.6 9.4 %copy-start.2 = (bf16[30,1024]{1,0:T(8,128)(2,1)S(1)}, bf16[30,1024]{1,0:T(8,128)(2,1)}, u32[]{:S(2)}) copy-start(bf16[30,1024]{1,0:T(8,128)(2,1)} %param.7) | copy-start | bytes 184324
  1.9 13.9 %all-to-all-start = ((s32[16,16,2]{1,2,0:T(2,128)}), s32[16,16,2]{1,2,0:T(2,128)S(1)}, u32[]{:S(2)}, u32[]{:S(2)}) async-start(s32[16,16,2]{1,2,0:T(2,128)} %broadcast_in_dim.133), calls=%async_computation | async-start | bytes 32768 | tf_op jit(solution)/shard_map/all_to_all | solution.py:152
  17.9 4.4 %copy-start = (bf16[30,1024]{1,0:T(8,128)(2,1)S(1)}, bf16[30,1024]{1,0:T(8,128)(2,1)}, u32[]{:S(2)}) copy-start(bf16[30,1024]{1,0:T(8,128)(2,1)} %x_ref.1) | copy-start | bytes 184324
  17.9 13.8 %all-to-all-start.1 = ((bf16[16,2,33,128]{3,1,2,0:T(2,128)(2,1)}), bf16[16,2,33,128]{3,1,2,0:T(2,128)(2,1)S(1)}, u32[]{:S(2)}, u32[]{:S(2)}) async-start(bf16[16,2,33,128]{3,1,2,0:T(2,128)(2,1)} %copy.88), calls=%async_computation.1 | async-start | bytes 540672 | tf_op jit(solution)/shard_map/all_to_all | solution.py:170
  21.6 0.7 copy-start.5
  32.1 0.7 copy-start.1
  45.5 13.5 %all-to-all-start.2 = ((f32[16,32,1,128]{3,2,1,0:T(1,128)}), f32[16,32,1,128]{3,2,1,0:T(1,128)S(1)}, u32[]{:S(2)}, u32[]{:S(2)}) async-start(f32[16,32,1,128]{3,2,1,0:T(1,128)} %shard_map.85), calls=%async_computation.2 | async-start | bytes 524288 | tf_op jit(solution)/shard_map/all_to_all | solution.py:231
  72.4 13.5 %all-to-all-start.3 = ((f32[16,32,1,128]{3,2,1,0:T(1,128)}), f32[16,32,1,128]{3,2,1,0:T(1,128)S(1)}, u32[]{:S(2)}, u32[]{:S(2)}) async-start(f32[16,32,1,128]{3,2,1,0:T(1,128)} %shard_map.86), calls=%async_computation.3 | async-start | bytes 524288 | tf_op jit(solution)/shard_map/all_to_all | solution.py:231
  86.7 0.7 copy-start.3

commit v7 on v5

--- a/solution.py
+++ b/solution.py
@@ -12,7 +12,7 @@
 
 floor_value = -1e30
 PADDED = 32
-CHUNK = 32
+CHUNK = 16
 TAIL = 16
 LOG2E = 1.4426950408889634
 LN2 = 0.6931471805599453

time: 96.7 us -> 98.3 us (1.017)
  Pallas kernels: 29.2 us -> 35 us
  starting transfers between devices: 22.1 us -> 18.1 us
    pallas_call x2, Pallas kernels: 19.8 us -> 23.8 us  [local(): sweep(flat_slots, pair_counts, source_rows, slot_coords, slot_potential -...]
    all_to_all x2, starting transfers between devices: 11 us -> 7.06 us  [local(): lax.all_to_all(lse, 'blocks', split_axis=0, concat_axis=0, tiled=True)]
    pallas_call x1, Pallas kernels: 9.41 us -> 11.2 us  [local(): final(flat_slots, pair_counts, source_rows, source_coords, slot_coords, s...]
where the time goes in v7:
time: 98.3 us; the launch traced here: 97.7 us
  Pallas kernels  35 us (36%)
  waiting for transfers between devices  33.3 us (34%)
  starting transfers between devices  18.1 us (18%)
  local copies, waits for them, and re-layouts  6.88 us (7%)
  other arithmetic  3.34 us (3%)
    pallas_call x2, Pallas kernels, local(): sweep(flat_slots, pair_counts, source_rows, slot_coords, slot_potential -...  23.8 us
    all_to_all x2, waiting for transfers between devices, local(): lax.all_to_all(lse, 'blocks', split_axis=0, concat_axis=0, tiled=True)  18.6 us
    pallas_call x1, Pallas kernels, local(): final(flat_slots, pair_counts, source_rows, source_coords, slot_coords, s...  11.2 us
    all_to_all x1, waiting for transfers between devices, local(): lax.all_to_all(send, 'blocks', split_axis=0, concat_axis=0, tiled=True)  9.07 us
    all_to_all x1, starting transfers between devices, local(): lax.all_to_all(jnp.broadcast_to(wanted[None], (peers, peers, cap)), 'bloc...  7.41 us
    all_to_all x2, starting transfers between devices, local(): lax.all_to_all(lse, 'blocks', split_axis=0, concat_axis=0, tiled=True)  7.06 us
    all_to_all x1, waiting for transfers between devices, local(): lax.all_to_all(jnp.broadcast_to(wanted[None], (peers, peers, cap)), 'bloc...  5.66 us
    all_to_all x1, starting transfers between devices, local(): lax.all_to_all(send, 'blocks', split_axis=0, concat_axis=0, tiled=True)  3.66 us
  transfers between devices with their start and end apart: 4, of which 4 were waited for; matrix products, arithmetic and copies ran while one was open for 3% of the time, Pallas kernels for 0%

profile of v7, /device:TPU:0, one launch (start us, length us, event | category | flops | bytes accessed | tf_op | source)
XLA Modules:
  0.0 97.7 jit_solution(7645281104338999870)
XLA Ops:
  0.6 0.0 copy-start.4
  0.6 0.0 copy-start.2
  0.7 0.7 copy-done.4
  1.3 0.6 broadcast_in_dim.133
  1.9 7.4 %all-to-all-start = ((s32[16,16,2]{1,2,0:T(2,128)}), s32[16,16,2]{1,2,0:T(2,128)S(1)}, u32[]{:S(2)}, u32[]{:S(2)}) async-start(s32[16,16,2]{1,2,0:T(2,128)} %broadcast_in_dim.133), calls=%async_computation | async-start | bytes 32768 | tf_op jit(solution)/shard_map/all_to_all | solution.py:152
  9.3 0.7 reduce-precision_convert_fusion.1
  10.1 0.0 copy-done.2
  10.2 5.7 %all-to-all-done = s32[16,16,2]{1,2,0:T(2,128)S(1)} async-done(((s32[16,16,2]{1,2,0:T(2,128)}), s32[16,16,2]{1,2,0:T(2,128)S(1)}, u32[]{:S(2)}, u32[]{:S(2)}) %all-to-all-start) | async-done | bytes 2080 | tf_op jit(solution)/shard_map/all_to_all | solution.py:152
  15.8 0.4 fusion.19
  16.3 0.1 squeeze.9
  16.4 0.6 gather_fusion
  17.0 0.9 copy.88
  17.9 0.0 copy-start
  17.9 3.7 %all-to-all-start.1 = ((bf16[16,2,33,128]{3,1,2,0:T(2,128)(2,1)}), bf16[16,2,33,128]{3,1,2,0:T(2,128)(2,1)S(1)}, u32[]{:S(2)}, u32[]{:S(2)}) async-start(bf16[16,2,33,128]{3,1,2,0:T(2,128)(2,1)} %copy.88), calls=%async_computation.1 | async-start | bytes 540672 | tf_op jit(solution)/shard_map/all_to_all | solution.py:170
  21.6 0.0 copy-start.5
  21.6 0.1 pad.4.clone
  21.7 0.1 pad.3.clone
  21.8 0.5 copy-done.5
  22.3 0.1 reshape.291.slots_ref
  22.4 0.0 copy-done
  22.4 0.2 copy.100
  22.6 0.1 concatenate.12.clone
  22.6 9.1 %all-to-all-done.1 = bf16[16,2,33,128]{3,1,2,0:T(2,128)(2,1)S(1)} async-done(((bf16[16,2,33,128]{3,1,2,0:T(2,128)(2,1)}), bf16[16,2,33,128]{3,1,2,0:T(2,128)(2,1)S(1)}, u32[]{:S(2)}, u32[]{:S(2)}) %all-to-all-start.1) | async-done | bytes 270368 | tf_op jit(solution)/shard_map/all_to_all | solution.py:170
  31.8 0.1 multiply_reduce_fusion
  32.0 0.1 maximum_maximum_fusion.y_ref
  32.1 0.0 copy-start.1
  32.1 0.6 copy-done.1
  32.8 11.9 %shard_map.85 = f32[16,32,1,128]{3,2,1,0:T(1,128)} custom-call(s32[256]{0:T(256)S(1)} %reshape.291.slots_ref, s32[8]{0:T(128)S(1)} %copy-done.1, bf16[8,128,32]{2,1,0:T(8,128)(2,1)S(1)} %bitcast.70, bf16[32,32,128]{2,1,0:T(8,128)(2,1)S(1)} %maximum_maximum_fusion.y_ref, f32[32,1,128]{2,1,0:T(1,128)S(1)} %get-tuple-element.11.h_ref, ...), custom_call_target="tpu_custom_call" | custom-call | tf_op jit(solution)/shard_map/pallas_call | solution.py:227
  44.7 3.5 %all-to-all-start.2 = ((f32[16,32,1,128]{3,2,1,0:T(1,128)}), f32[16,32,1,128]{3,2,1,0:T(1,128)S(1)}, u32[]{:S(2)}, u32[]{:S(2)}) async-start(f32[16,32,1,128]{3,2,1,0:T(1,128)} %shard_map.85), calls=%async_computation.2 | async-start | bytes 524288 | tf_op jit(solution)/shard_map/all_to_all | solution.py:231
  48.2 0.1 copy.91
  48.3 0.1 copy.90
  48.4 0.1 copy.95
  48.5 0.1 broadcast_compare_fusion
  48.6 9.6 %all-to-all-done.2 = f32[16,32,1,128]{3,2,1,0:T(1,128)S(1)} async-done(((f32[16,32,1,128]{3,2,1,0:T(1,128)}), f32[16,32,1,128]{3,2,1,0:T(1,128)S(1)}, u32[]{:S(2)}, u32[]{:S(2)}) %all-to-all-start.2) | async-done | bytes 262176 | tf_op jit(solution)/shard_map/all_to_all | solution.py:231
  58.2 0.2 copy.92
  58.3 0.2 select_reduce_fusion.3
  58.6 0.3 select_reduce_fusion.2
  58.8 0.1 fusion.17
  58.9 11.9 %shard_map.86 = f32[16,32,1,128]{3,2,1,0:T(1,128)} custom-call(s32[256]{0:T(256)S(1)} %reshape.291.slots_ref, s32[8]{0:T(128)S(1)} %copy-done.1, bf16[8,128,32]{2,1,0:T(8,128)(2,1)S(1)} %bitcast.71, bf16[32,32,128]{2,1,0:T(8,128)(2,1)S(1)} %maximum_maximum_fusion.y_ref, f32[32,1,128]{2,1,0:T(1,128)S(1)} %get-tuple-element.9.h_ref, ...), custom_call_target="tpu_custom_call" | custom-call | tf_op jit(solution)/shard_map/pallas_call | solution.py:227
  70.8 3.5 %all-to-all-start.3 = ((f32[16,32,1,128]{3,2,1,0:T(1,128)}), f32[16,32,1,128]{3,2,1,0:T(1,128)S(1)}, u32[]{:S(2)}, u32[]{:S(2)}) async-start(f32[16,32,1,128]{3,2,1,0:T(1,128)} %shard_map.86), calls=%async_computation.3 | async-start | bytes 524288 | tf_op jit(solution)/shard_map/all_to_all | solution.py:231
  74.4 0.1 fusion.20
  74.5 0.5 copy.101
  75.0 0.3 concatenate.15.clone.yT_ref
  75.3 9.0 %all-to-all-done.3 = f32[16,32,1,128]{3,2,1,0:T(1,128)S(1)} async-done(((f32[16,32,1,128]{3,2,1,0:T(1,128)}), f32[16,32,1,128]{3,2,1,0:T(1,128)S(1)}, u32[]{:S(2)}, u32[]{:S(2)}) %all-to-all-start.3) | async-done | bytes 262176 | tf_op jit(solution)/shard_map/all_to_all | solution.py:231
  84.3 0.1 select_reduce_fusion.7
  84.5 0.1 select_reduce_fusion.6
  84.6 0.1 select_reduce_fusion.4
  84.7 0.2 copy.93
  84.9 0.2 select_reduce_fusion.1
  85.1 0.0 copy-start.3
  85.1 0.3 select_reduce_fusion
  85.4 0.4 copy-done.3
  85.8 0.6 fusion.10
  86.4 0.1 fusion.4.h_ref
  86.5 11.2 %shard_map.87 = (f32[8,1,128]{2,1,0:T(1,128)}, f32[30,1024]{1,0:T(8,128)}) custom-call(s32[256]{0:T(256)S(1)} %reshape.291.slots_ref, s32[8]{0:T(128)S(1)} %copy-done.1, bf16[8,128,32]{2,1,0:T(8,128)(2,1)S(1)} %bitcast.72, bf16[30,1024]{1,0:T(8,128)(2,1)S(1)} %copy-done, bf16[32,32,128]{2,1,0:T(8,128)(2,1)S(1)} %maximum_maximum_fusion.y_ref, ...), custom_call_target="tpu_custom_call" | custom-call | tf_op jit(solution)/shard_map/pallas_call | solution.py:248
  (20 shorter events, 0.3 us)
Async XLA Ops:
  0.6 0.7 copy-start.4
  0.6 9.4 %copy-start.2 = (bf16[30,1024]{1,0:T(8,128)(2,1)S(1)}, bf16[30,1024]{1,0:T(8,128)(2,1)}, u32[]{:S(2)}) copy-start(bf16[30,1024]{1,0:T(8,128)(2,1)} %param.7) | copy-start | bytes 184324
  1.9 13.9 %all-to-all-start = ((s32[16,16,2]{1,2,0:T(2,128)}), s32[16,16,2]{1,2,0:T(2,128)S(1)}, u32[]{:S(2)}, u32[]{:S(2)}) async-start(s32[16,16,2]{1,2,0:T(2,128)} %broadcast_in_dim.133), calls=%async_computation | async-start | bytes 32768 | tf_op jit(solution)/shard_map/all_to_all | solution.py:152
  17.9 4.4 %copy-start = (bf16[30,1024]{1,0:T(8,128)(2,1)S(1)}, bf16[30,1024]{1,0:T(8,128)(2,1)}, u32[]{:S(2)}) copy-start(bf16[30,1024]{1,0:T(8,128)(2,1)} %x_ref.1) | copy-start | bytes 184324
  17.9 13.8 %all-to-all-start.1 = ((bf16[16,2,33,128]{3,1,2,0:T(2,128)(2,1)}), bf16[16,2,33,128]{3,1,2,0:T(2,128)(2,1)S(1)}, u32[]{:S(2)}, u32[]{:S(2)}) async-start(bf16[16,2,33,128]{3,1,2,0:T(2,128)(2,1)} %copy.88), calls=%async_computation.1 | async-start | bytes 540672 | tf_op jit(solution)/shard_map/all_to_all | solution.py:170
  21.6 0.7 copy-start.5
  32.1 0.7 copy-start.1
  44.7 13.5 %all-to-all-start.2 = ((f32[16,32,1,128]{3,2,1,0:T(1,128)}), f32[16,32,1,128]{3,2,1,0:T(1,128)S(1)}, u32[]{:S(2)}, u32[]{:S(2)}) async-start(f32[16,32,1,128]{3,2,1,0:T(1,128)} %shard_map.85), calls=%async_computation.2 | async-start | bytes 524288 | tf_op jit(solution)/shard_map/all_to_all | solution.py:231
  70.8 13.5 %all-to-all-start.3 = ((f32[16,32,1,128]{3,2,1,0:T(1,128)}), f32[16,32,1,128]{3,2,1,0:T(1,128)S(1)}, u32[]{:S(2)}, u32[]{:S(2)}) async-start(f32[16,32,1,128]{3,2,1,0:T(1,128)} %shard_map.86), calls=%async_computation.3 | async-start | bytes 524288 | tf_op jit(solution)/shard_map/all_to_all | solution.py:231
  85.1 0.7 copy-start.3
